TPU v7x, 512 devices: a whole 4x4x16 slice. The times are simulated.
512 devices in a mesh: ctx: 16 (over y, x_hi, core), ch: 32 (over z, x_lo).
Axes of the slice: x: 4 (x_hi: 2, x_lo: 2; x = x_hi * 2 + x_lo), y: 4, z: 16, core: 2. Of those that a mesh axis runs over, the one named last changes fastest.
Arguments:
- query: bfloat16 [512, 16384], P('ch', 'ctx'), may hold values from -16 to 16
- key_branch: bfloat16 [512, 16384], P('ch', 'ctx'), may hold values from -6 to 6
- value_branch: bfloat16 [512, 16384], P('ch', 'ctx'), may hold values from -6 to 6
- residue: float32 [512, 16], P('ch'), may hold values from -1.5 to 1.5
- rate: float32 [512, 16], P('ch'), may hold values from 1.5258789e-05 to 0.03
- skip: float32 [512], P('ch'), may hold values from -4 to 4
- gain: float32 [512], P('ch'), may hold values from 0.1 to 1.9
Outputs:
- mixed_out: bfloat16 [512, 16384], P('ch', 'ctx')
All inputs are finite; a program needn't handle non-finite values.
Results may differ from a plain program's by a relative error of at most 0.009.
Values may be sent and summed in bfloat16 or wider, within the bound.
No kernel may reach another device: no remote copies, remote signals or barrier semaphores. Data moves between devices by JAX's collectives and lax.ppermute only.
A program may use at most 64 MiB of HBM per device.

v0:
```python
import math

import jax
import jax.numpy as jnp
from jax import lax
from jax.sharding import PartitionSpec as P


def shifted(block, axis, distance):
    devices = range(lax.axis_size(axis))
    route = [(i - distance, i) for i in devices if i - distance in devices]
    return lax.ppermute(block, axis, route)


def modal_taps(lags, residue, rate):
    lag_float = jnp.maximum(lags, 0).astype(jnp.float32)
    scaled = jnp.sqrt(-jnp.expm1(-2.0 * rate)) * residue

    def add_mode(index, total):
        return total + scaled[:, index][:, None] * jnp.exp(
            -rate[:, index][:, None] * lag_float[None, :]
        )

    start_total = jnp.zeros((residue.shape[0], lags.shape[0]), jnp.float32)
    total = lax.fori_loop(0, residue.shape[1], add_mode, start_total)
    return jnp.where((lags >= 0)[None, :], total, 0.0)


def angle_table(count_a, count_b, period):
    first = jnp.arange(count_a, dtype=jnp.int32)[:, None]
    second = jnp.arange(count_b, dtype=jnp.int32)[None, :]
    angle = 2.0 * math.pi / period * (first * second % period).astype(jnp.float32)
    return (jnp.cos(angle), jnp.sin(angle))


def make_tables(points):
    outer = points // 128
    cos_outer, sin_outer = angle_table(outer, outer, outer)
    twist_cos, twist_sin = angle_table(outer, 128, points)
    cos_inner, sin_inner = angle_table(128, 128, 128)
    return (cos_outer, sin_outer, twist_cos, twist_sin, cos_inner, sin_inner)


def spectrum_of(signal, tables, level):
    cos_outer, sin_outer, twist_cos, twist_sin, cos_inner, sin_inner = tables
    row_count = signal.shape[0]
    outer = cos_outer.shape[0]
    cube_rows = signal.reshape(row_count, outer, 128)
    first_real = jnp.einsum("rnq,nk->rkq", cube_rows, cos_outer, precision=level)
    first_imag = -jnp.einsum("rnq,nk->rkq", cube_rows, sin_outer, precision=level)
    turned_real = first_real * twist_cos + first_imag * twist_sin
    turned_imag = first_imag * twist_cos - first_real * twist_sin
    spec_real = jnp.einsum("rkq,qm->rkm", turned_real, cos_inner, precision=level) + jnp.einsum(
        "rkq,qm->rkm", turned_imag, sin_inner, precision=level
    )
    spec_imag = jnp.einsum("rkq,qm->rkm", turned_imag, cos_inner, precision=level) - jnp.einsum(
        "rkq,qm->rkm", turned_real, sin_inner, precision=level
    )
    return (spec_real, spec_imag)


def spectrum_back(spec_real, spec_imag, tables):
    cos_outer, sin_outer, twist_cos, twist_sin, cos_inner, sin_inner = tables
    row_count = spec_real.shape[0]
    outer = cos_outer.shape[0]
    level = lax.Precision.HIGH
    inner_real = jnp.einsum("rkm,mq->rkq", spec_real, cos_inner, precision=level) - jnp.einsum(
        "rkm,mq->rkq", spec_imag, sin_inner, precision=level
    )
    inner_imag = jnp.einsum("rkm,mq->rkq", spec_imag, cos_inner, precision=level) + jnp.einsum(
        "rkm,mq->rkq", spec_real, sin_inner, precision=level
    )
    turned_real = inner_real * twist_cos - inner_imag * twist_sin
    turned_imag = inner_imag * twist_cos + inner_real * twist_sin
    result = jnp.einsum("rkq,kn->rnq", turned_real, cos_outer, precision=level) - jnp.einsum(
        "rkq,kn->rnq", turned_imag, sin_outer, precision=level
    )
    return result.reshape(row_count, outer * 128) / (outer * 128.0)


def padded_spectrum(block, tables):
    block_float = block.astype(jnp.float32)
    padded = jnp.concatenate([block_float, jnp.zeros_like(block_float)], axis=1)
    return spectrum_of(padded, tables, lax.Precision.HIGH)


def body(query, key_branch, value_branch, residue, rate, skip, gain):
    signal = key_branch * value_branch
    ctx_count = lax.axis_size("ctx")
    position = lax.axis_index("ctx")
    block_len = signal.shape[1]
    points = 2 * block_len
    tables = make_tables(points)
    base_lags = jnp.arange(points, dtype=jnp.int32) - block_len

    def lag_spectrum(offset, rows_residue, rows_rate):
        lags = base_lags + offset * block_len
        return spectrum_of(modal_taps(lags, rows_residue, rows_rate), tables, lax.Precision.HIGHEST)

    own_real, own_imag = padded_spectrum(signal, tables)
    filt_real, filt_imag = lag_spectrum(0, residue, rate)
    start_real = filt_real * own_real - filt_imag * own_imag
    start_imag = filt_real * own_imag + filt_imag * own_real

    def add_remote(offset, state):
        moving, total_real, total_imag = state
        moving = shifted(moving, "ctx", 1)
        moving_real, moving_imag = padded_spectrum(moving, tables)
        lag_real, lag_imag = lag_spectrum(offset, residue, rate)
        valid = (position >= offset).astype(jnp.float32)
        total_real = total_real + valid * (lag_real * moving_real - lag_imag * moving_imag)
        total_imag = total_imag + valid * (lag_real * moving_imag + lag_imag * moving_real)
        return (moving, total_real, total_imag)

    final_state = lax.fori_loop(1, ctx_count, add_remote, (signal, start_real, start_imag))
    total_real, total_imag = (final_state[1], final_state[2])
    conv = spectrum_back(total_real, total_imag, tables)[:, block_len:]
    signal_float = signal.astype(jnp.float32)
    mixed = query.astype(jnp.float32) * (conv + skip[:, None] * signal_float)
    channel_total = signal.shape[0] * lax.axis_size("ch")
    square_sum = lax.psum(jnp.sum(mixed * mixed, axis=0), "ch")
    scale_rows = 1.0 / jnp.sqrt(square_sum / channel_total + 1e-06)
    return (mixed * scale_rows[None, :] * gain[:, None]).astype(jnp.bfloat16)


def solution(mesh):
    placed = (
        P("ch", "ctx"),
        P("ch", "ctx"),
        P("ch", "ctx"),
        P("ch", None),
        P("ch", None),
        P("ch"),
        P("ch"),
    )
    return jax.shard_map(
        body, mesh=mesh, in_specs=placed, out_specs=P("ch", "ctx"), check_vma=False
    )
```

profile of v0, /device:TPU:4, one launch (start us, length us, event | category | flops | bytes accessed | tf_op | source)
XLA Modules:
  0.0 246.8 jit_solution(11521594074968233466)
XLA Ops:
  0.0 0.7 copy-done.3
  0.9 0.5 copy-done.2
  4.0 2.7 %while.63 = (s32[]{:T(128)}, f32[16,2048]{1,0:T(8,128)S(1)}, f32[16,16]{0,1:T(8,128)S(1)}, f32[16,16]{0,1:T(8,128)S(1)}, s32[]{:T(128)}, /*index=5*/s32[]{:T(128)}) while((s32[]{:T(128)}, f32[16,2048]{1,0:T(8,128)S(1)}, f32[16,16]{0,1:T(8,128)S(1)}, f32[16,16]{0,1:T(8,128)S(1)}, s32[]{:T(128)}, /*index=5*/s32[]{:T(128)}) %tuple.116), condition=%wide.region_1.2_spmd.clone, body=%wide.region_0.1_spmd.clone.sunk | while | flops 137235 | bytes 279003 | solution.py:25
  7.3 0.5 fusion.128
  7.9 0.5 fusion.132
  8.9 0.5 multiply_add_fusion.8
  9.5 162.7 %while.62 = (s32[]{:T(128)}, bf16[16,1024]{1,0:T(8,128)(2,1)S(1)}, f32[16,16,128]{2,1,0:T(8,128)S(1)}, f32[16,16,128]{2,1,0:T(8,128)S(1)}, s32[]{:T(128)}, /*ind...) while((s32[]{:T(128)}, bf16[16,1024]{1,0:T(8,128)(2,1)S(1)}, ...), condition=%wide.region_5.6_spmd.clone.clone, body=%wide.region_2.5_spmd.clone.clone.sunk | while | flops 324231936 | bytes 6758118 | solution.py:115
  9.5 1.9 collective-permute-start
  11.5 2.5 while.64
  14.7 0.5 fusion.340
  18.6 0.6 multiply_add_fusion.22
  19.2 3.5 %collective-permute-start = (bf16[16,1024]{1,0:T(8,128)(2,1)S(1)}, bf16[16,1024]{1,0:T(8,128)(2,1)S(1)}, u32[]{:S(2)}, u32[]{:S(2)}) collective-permute-start(bf16[16,1024]{1,0:T(8,128)(2,1)S(1)} %get-tuple-element.838), channel_id=1, source_target_pairs={{0,32},{32,64},{64,96},{96,128},{128,160},{160,192},{192,224},{224... | collective-permute-start | bytes 98312 | tf_op jit(solution)/shard_map/while/body/eval_jaxpr/ppermute | solution.py:12
  22.9 2.5 while.64
  26.0 0.5 fusion.340
  27.1 0.5 fusion.342
  30.0 0.6 multiply_add_fusion.22
  30.6 2.7 %collective-permute-start = (bf16[16,1024]{1,0:T(8,128)(2,1)S(1)}, bf16[16,1024]{1,0:T(8,128)(2,1)S(1)}, u32[]{:S(2)}, u32[]{:S(2)}) collective-permute-start(bf16[16,1024]{1,0:T(8,128)(2,1)S(1)} %get-tuple-element.838), channel_id=1, source_target_pairs={{0,32},{32,64},{64,96},{96,128},{128,160},{160,192},{192,224},{224... | collective-permute-start | bytes 98312 | tf_op jit(solution)/shard_map/while/body/eval_jaxpr/ppermute | solution.py:12
  33.5 2.5 while.64
  36.6 0.5 fusion.340
  40.5 0.6 multiply_add_fusion.22
  41.2 4.2 %collective-permute-start = (bf16[16,1024]{1,0:T(8,128)(2,1)S(1)}, bf16[16,1024]{1,0:T(8,128)(2,1)S(1)}, u32[]{:S(2)}, u32[]{:S(2)}) collective-permute-start(bf16[16,1024]{1,0:T(8,128)(2,1)S(1)} %get-tuple-element.838), channel_id=1, source_target_pairs={{0,32},{32,64},{64,96},{96,128},{128,160},{160,192},{192,224},{224... | collective-permute-start | bytes 98312 | tf_op jit(solution)/shard_map/while/body/eval_jaxpr/ppermute | solution.py:12
  45.5 2.5 while.64
  48.7 0.5 fusion.340
  52.6 0.6 multiply_add_fusion.22
  53.2 2.7 %collective-permute-start = (bf16[16,1024]{1,0:T(8,128)(2,1)S(1)}, bf16[16,1024]{1,0:T(8,128)(2,1)S(1)}, u32[]{:S(2)}, u32[]{:S(2)}) collective-permute-start(bf16[16,1024]{1,0:T(8,128)(2,1)S(1)} %get-tuple-element.838), channel_id=1, source_target_pairs={{0,32},{32,64},{64,96},{96,128},{128,160},{160,192},{192,224},{224... | collective-permute-start | bytes 98312 | tf_op jit(solution)/shard_map/while/body/eval_jaxpr/ppermute | solution.py:12
  56.1 2.5 while.64
  59.3 0.5 fusion.340
  63.2 0.6 multiply_add_fusion.22
  63.8 2.7 %collective-permute-start = (bf16[16,1024]{1,0:T(8,128)(2,1)S(1)}, bf16[16,1024]{1,0:T(8,128)(2,1)S(1)}, u32[]{:S(2)}, u32[]{:S(2)}) collective-permute-start(bf16[16,1024]{1,0:T(8,128)(2,1)S(1)} %get-tuple-element.838), channel_id=1, source_target_pairs={{0,32},{32,64},{64,96},{96,128},{128,160},{160,192},{192,224},{224... | collective-permute-start | bytes 98312 | tf_op jit(solution)/shard_map/while/body/eval_jaxpr/ppermute | solution.py:12
  66.7 2.5 while.64
  73.7 0.6 multiply_add_fusion.22
  74.4 2.7 %collective-permute-start = (bf16[16,1024]{1,0:T(8,128)(2,1)S(1)}, bf16[16,1024]{1,0:T(8,128)(2,1)S(1)}, u32[]{:S(2)}, u32[]{:S(2)}) collective-permute-start(bf16[16,1024]{1,0:T(8,128)(2,1)S(1)} %get-tuple-element.838), channel_id=1, source_target_pairs={{0,32},{32,64},{64,96},{96,128},{128,160},{160,192},{192,224},{224... | collective-permute-start | bytes 98312 | tf_op jit(solution)/shard_map/while/body/eval_jaxpr/ppermute | solution.py:12
  77.3 2.5 while.64
  84.3 0.6 multiply_add_fusion.22
  85.0 4.2 %collective-permute-start = (bf16[16,1024]{1,0:T(8,128)(2,1)S(1)}, bf16[16,1024]{1,0:T(8,128)(2,1)S(1)}, u32[]{:S(2)}, u32[]{:S(2)}) collective-permute-start(bf16[16,1024]{1,0:T(8,128)(2,1)S(1)} %get-tuple-element.838), channel_id=1, source_target_pairs={{0,32},{32,64},{64,96},{96,128},{128,160},{160,192},{192,224},{224... | collective-permute-start | bytes 98312 | tf_op jit(solution)/shard_map/while/body/eval_jaxpr/ppermute | solution.py:12
  89.3 2.5 while.64
  96.3 0.6 multiply_add_fusion.22
  97.0 2.8 %collective-permute-start = (bf16[16,1024]{1,0:T(8,128)(2,1)S(1)}, bf16[16,1024]{1,0:T(8,128)(2,1)S(1)}, u32[]{:S(2)}, u32[]{:S(2)}) collective-permute-start(bf16[16,1024]{1,0:T(8,128)(2,1)S(1)} %get-tuple-element.838), channel_id=1, source_target_pairs={{0,32},{32,64},{64,96},{96,128},{128,160},{160,192},{192,224},{224... | collective-permute-start | bytes 98312 | tf_op jit(solution)/shard_map/while/body/eval_jaxpr/ppermute | solution.py:12
  99.9 2.5 while.64
  106.9 0.6 multiply_add_fusion.22
  107.5 2.7 %collective-permute-start = (bf16[16,1024]{1,0:T(8,128)(2,1)S(1)}, bf16[16,1024]{1,0:T(8,128)(2,1)S(1)}, u32[]{:S(2)}, u32[]{:S(2)}) collective-permute-start(bf16[16,1024]{1,0:T(8,128)(2,1)S(1)} %get-tuple-element.838), channel_id=1, source_target_pairs={{0,32},{32,64},{64,96},{96,128},{128,160},{160,192},{192,224},{224... | collective-permute-start | bytes 98312 | tf_op jit(solution)/shard_map/while/body/eval_jaxpr/ppermute | solution.py:12
  110.4 2.5 while.64
  113.6 0.5 fusion.340
  117.5 0.6 multiply_add_fusion.22
  118.1 2.7 %collective-permute-start = (bf16[16,1024]{1,0:T(8,128)(2,1)S(1)}, bf16[16,1024]{1,0:T(8,128)(2,1)S(1)}, u32[]{:S(2)}, u32[]{:S(2)}) collective-permute-start(bf16[16,1024]{1,0:T(8,128)(2,1)S(1)} %get-tuple-element.838), channel_id=1, source_target_pairs={{0,32},{32,64},{64,96},{96,128},{128,160},{160,192},{192,224},{224... | collective-permute-start | bytes 98312 | tf_op jit(solution)/shard_map/while/body/eval_jaxpr/ppermute | solution.py:12
  121.0 2.5 while.64
  128.1 0.6 multiply_add_fusion.22
  128.7 3.9 %collective-permute-start = (bf16[16,1024]{1,0:T(8,128)(2,1)S(1)}, bf16[16,1024]{1,0:T(8,128)(2,1)S(1)}, u32[]{:S(2)}, u32[]{:S(2)}) collective-permute-start(bf16[16,1024]{1,0:T(8,128)(2,1)S(1)} %get-tuple-element.838), channel_id=1, source_target_pairs={{0,32},{32,64},{64,96},{96,128},{128,160},{160,192},{192,224},{224... | collective-permute-start | bytes 98312 | tf_op jit(solution)/shard_map/while/body/eval_jaxpr/ppermute | solution.py:12
  132.7 2.5 while.64
  139.8 0.6 multiply_add_fusion.22
  140.4 2.8 %collective-permute-start = (bf16[16,1024]{1,0:T(8,128)(2,1)S(1)}, bf16[16,1024]{1,0:T(8,128)(2,1)S(1)}, u32[]{:S(2)}, u32[]{:S(2)}) collective-permute-start(bf16[16,1024]{1,0:T(8,128)(2,1)S(1)} %get-tuple-element.838), channel_id=1, source_target_pairs={{0,32},{32,64},{64,96},{96,128},{128,160},{160,192},{192,224},{224... | collective-permute-start | bytes 98312 | tf_op jit(solution)/shard_map/while/body/eval_jaxpr/ppermute | solution.py:12
  143.3 2.5 while.64
  150.4 0.6 multiply_add_fusion.22
  151.0 2.8 %collective-permute-start = (bf16[16,1024]{1,0:T(8,128)(2,1)S(1)}, bf16[16,1024]{1,0:T(8,128)(2,1)S(1)}, u32[]{:S(2)}, u32[]{:S(2)}) collective-permute-start(bf16[16,1024]{1,0:T(8,128)(2,1)S(1)} %get-tuple-element.838), channel_id=1, source_target_pairs={{0,32},{32,64},{64,96},{96,128},{128,160},{160,192},{192,224},{224... | collective-permute-start | bytes 98312 | tf_op jit(solution)/shard_map/while/body/eval_jaxpr/ppermute | solution.py:12
  153.9 2.5 while.64
  161.0 0.6 multiply_add_fusion.22
  161.6 2.7 %collective-permute-start = (bf16[16,1024]{1,0:T(8,128)(2,1)S(1)}, bf16[16,1024]{1,0:T(8,128)(2,1)S(1)}, u32[]{:S(2)}, u32[]{:S(2)}) collective-permute-start(bf16[16,1024]{1,0:T(8,128)(2,1)S(1)} %get-tuple-element.838), channel_id=1, source_target_pairs={{0,32},{32,64},{64,96},{96,128},{128,160},{160,192},{192,224},{224... | collective-permute-start | bytes 98312 | tf_op jit(solution)/shard_map/while/body/eval_jaxpr/ppermute | solution.py:12
  164.5 2.5 while.64
  167.6 0.5 fusion.340
  171.6 0.6 multiply_add_fusion.22
  174.6 0.7 copy-done
  175.4 70.1 %psum.7 = f32[1024]{0:T(1024)S(1)} all-reduce(f32[1024]{0:T(1024)S(1)} %multiply_reduce_fusion), channel_id=1, replica_groups=mesh['ctx'=16,'ch'=32] {'ch'}, use_global_device_ids=true, to_apply=%region_7.8 | all-reduce | flops 1024 | bytes 8192 | tf_op jit(solution)/shard_map/psum | solution.py:121
  245.5 0.6 copy-done.6
  246.1 0.7 multiply_convert_fusion
  (890 shorter events, 103.1 us)
Async XLA Ops:
  0.0 0.7 copy-start.3
  0.0 0.8 copy-start.4
  0.7 0.8 copy-start.2
  0.8 0.8 copy-start.1
  9.5 6.8 %collective-permute-start = (bf16[16,1024]{1,0:T(8,128)(2,1)S(1)}, bf16[16,1024]{1,0:T(8,128)(2,1)S(1)}, u32[]{:S(2)}, u32[]{:S(2)}) collective-permute-start(bf16[16,1024]{1,0:T(8,128)(2,1)S(1)} %get-tuple-element.838), channel_id=1, source_target_pairs={{0,32},{32,64},{64,96},{96,128},{128,160},{160,192},{192,224},{224... | collective-permute-start | bytes 98312 | tf_op jit(solution)/shard_map/while/body/eval_jaxpr/ppermute | solution.py:12
  19.2 8.4 %collective-permute-start = (bf16[16,1024]{1,0:T(8,128)(2,1)S(1)}, bf16[16,1024]{1,0:T(8,128)(2,1)S(1)}, u32[]{:S(2)}, u32[]{:S(2)}) collective-permute-start(bf16[16,1024]{1,0:T(8,128)(2,1)S(1)} %get-tuple-element.838), channel_id=1, source_target_pairs={{0,32},{32,64},{64,96},{96,128},{128,160},{160,192},{192,224},{224... | collective-permute-start | bytes 98312 | tf_op jit(solution)/shard_map/while/body/eval_jaxpr/ppermute | solution.py:12
  30.6 7.6 %collective-permute-start = (bf16[16,1024]{1,0:T(8,128)(2,1)S(1)}, bf16[16,1024]{1,0:T(8,128)(2,1)S(1)}, u32[]{:S(2)}, u32[]{:S(2)}) collective-permute-start(bf16[16,1024]{1,0:T(8,128)(2,1)S(1)} %get-tuple-element.838), channel_id=1, source_target_pairs={{0,32},{32,64},{64,96},{96,128},{128,160},{160,192},{192,224},{224... | collective-permute-start | bytes 98312 | tf_op jit(solution)/shard_map/while/body/eval_jaxpr/ppermute | solution.py:12
  41.2 9.1 %collective-permute-start = (bf16[16,1024]{1,0:T(8,128)(2,1)S(1)}, bf16[16,1024]{1,0:T(8,128)(2,1)S(1)}, u32[]{:S(2)}, u32[]{:S(2)}) collective-permute-start(bf16[16,1024]{1,0:T(8,128)(2,1)S(1)} %get-tuple-element.838), channel_id=1, source_target_pairs={{0,32},{32,64},{64,96},{96,128},{128,160},{160,192},{192,224},{224... | collective-permute-start | bytes 98312 | tf_op jit(solution)/shard_map/while/body/eval_jaxpr/ppermute | solution.py:12
  53.2 7.6 %collective-permute-start = (bf16[16,1024]{1,0:T(8,128)(2,1)S(1)}, bf16[16,1024]{1,0:T(8,128)(2,1)S(1)}, u32[]{:S(2)}, u32[]{:S(2)}) collective-permute-start(bf16[16,1024]{1,0:T(8,128)(2,1)S(1)} %get-tuple-element.838), channel_id=1, source_target_pairs={{0,32},{32,64},{64,96},{96,128},{128,160},{160,192},{192,224},{224... | collective-permute-start | bytes 98312 | tf_op jit(solution)/shard_map/while/body/eval_jaxpr/ppermute | solution.py:12
  63.8 7.6 %collective-permute-start = (bf16[16,1024]{1,0:T(8,128)(2,1)S(1)}, bf16[16,1024]{1,0:T(8,128)(2,1)S(1)}, u32[]{:S(2)}, u32[]{:S(2)}) collective-permute-start(bf16[16,1024]{1,0:T(8,128)(2,1)S(1)} %get-tuple-element.838), channel_id=1, source_target_pairs={{0,32},{32,64},{64,96},{96,128},{128,160},{160,192},{192,224},{224... | collective-permute-start | bytes 98312 | tf_op jit(solution)/shard_map/while/body/eval_jaxpr/ppermute | solution.py:12
  74.4 7.6 %collective-permute-start = (bf16[16,1024]{1,0:T(8,128)(2,1)S(1)}, bf16[16,1024]{1,0:T(8,128)(2,1)S(1)}, u32[]{:S(2)}, u32[]{:S(2)}) collective-permute-start(bf16[16,1024]{1,0:T(8,128)(2,1)S(1)} %get-tuple-element.838), channel_id=1, source_target_pairs={{0,32},{32,64},{64,96},{96,128},{128,160},{160,192},{192,224},{224... | collective-permute-start | bytes 98312 | tf_op jit(solution)/shard_map/while/body/eval_jaxpr/ppermute | solution.py:12
  85.0 9.0 %collective-permute-start = (bf16[16,1024]{1,0:T(8,128)(2,1)S(1)}, bf16[16,1024]{1,0:T(8,128)(2,1)S(1)}, u32[]{:S(2)}, u32[]{:S(2)}) collective-permute-start(bf16[16,1024]{1,0:T(8,128)(2,1)S(1)} %get-tuple-element.838), channel_id=1, source_target_pairs={{0,32},{32,64},{64,96},{96,128},{128,160},{160,192},{192,224},{224... | collective-permute-start | bytes 98312 | tf_op jit(solution)/shard_map/while/body/eval_jaxpr/ppermute | solution.py:12
  97.0 7.6 %collective-permute-start = (bf16[16,1024]{1,0:T(8,128)(2,1)S(1)}, bf16[16,1024]{1,0:T(8,128)(2,1)S(1)}, u32[]{:S(2)}, u32[]{:S(2)}) collective-permute-start(bf16[16,1024]{1,0:T(8,128)(2,1)S(1)} %get-tuple-element.838), channel_id=1, source_target_pairs={{0,32},{32,64},{64,96},{96,128},{128,160},{160,192},{192,224},{224... | collective-permute-start | bytes 98312 | tf_op jit(solution)/shard_map/while/body/eval_jaxpr/ppermute | solution.py:12
  107.5 7.6 %collective-permute-start = (bf16[16,1024]{1,0:T(8,128)(2,1)S(1)}, bf16[16,1024]{1,0:T(8,128)(2,1)S(1)}, u32[]{:S(2)}, u32[]{:S(2)}) collective-permute-start(bf16[16,1024]{1,0:T(8,128)(2,1)S(1)} %get-tuple-element.838), channel_id=1, source_target_pairs={{0,32},{32,64},{64,96},{96,128},{128,160},{160,192},{192,224},{224... | collective-permute-start | bytes 98312 | tf_op jit(solution)/shard_map/while/body/eval_jaxpr/ppermute | solution.py:12
  118.1 7.6 %collective-permute-start = (bf16[16,1024]{1,0:T(8,128)(2,1)S(1)}, bf16[16,1024]{1,0:T(8,128)(2,1)S(1)}, u32[]{:S(2)}, u32[]{:S(2)}) collective-permute-start(bf16[16,1024]{1,0:T(8,128)(2,1)S(1)} %get-tuple-element.838), channel_id=1, source_target_pairs={{0,32},{32,64},{64,96},{96,128},{128,160},{160,192},{192,224},{224... | collective-permute-start | bytes 98312 | tf_op jit(solution)/shard_map/while/body/eval_jaxpr/ppermute | solution.py:12
  128.7 8.8 %collective-permute-start = (bf16[16,1024]{1,0:T(8,128)(2,1)S(1)}, bf16[16,1024]{1,0:T(8,128)(2,1)S(1)}, u32[]{:S(2)}, u32[]{:S(2)}) collective-permute-start(bf16[16,1024]{1,0:T(8,128)(2,1)S(1)} %get-tuple-element.838), channel_id=1, source_target_pairs={{0,32},{32,64},{64,96},{96,128},{128,160},{160,192},{192,224},{224... | collective-permute-start | bytes 98312 | tf_op jit(solution)/shard_map/while/body/eval_jaxpr/ppermute | solution.py:12
  140.4 7.6 %collective-permute-start = (bf16[16,1024]{1,0:T(8,128)(2,1)S(1)}, bf16[16,1024]{1,0:T(8,128)(2,1)S(1)}, u32[]{:S(2)}, u32[]{:S(2)}) collective-permute-start(bf16[16,1024]{1,0:T(8,128)(2,1)S(1)} %get-tuple-element.838), channel_id=1, source_target_pairs={{0,32},{32,64},{64,96},{96,128},{128,160},{160,192},{192,224},{224... | collective-permute-start | bytes 98312 | tf_op jit(solution)/shard_map/while/body/eval_jaxpr/ppermute | solution.py:12
  151.0 7.6 %collective-permute-start = (bf16[16,1024]{1,0:T(8,128)(2,1)S(1)}, bf16[16,1024]{1,0:T(8,128)(2,1)S(1)}, u32[]{:S(2)}, u32[]{:S(2)}) collective-permute-start(bf16[16,1024]{1,0:T(8,128)(2,1)S(1)} %get-tuple-element.838), channel_id=1, source_target_pairs={{0,32},{32,64},{64,96},{96,128},{128,160},{160,192},{192,224},{224... | collective-permute-start | bytes 98312 | tf_op jit(solution)/shard_map/while/body/eval_jaxpr/ppermute | solution.py:12
  161.6 7.6 %collective-permute-start = (bf16[16,1024]{1,0:T(8,128)(2,1)S(1)}, bf16[16,1024]{1,0:T(8,128)(2,1)S(1)}, u32[]{:S(2)}, u32[]{:S(2)}) collective-permute-start(bf16[16,1024]{1,0:T(8,128)(2,1)S(1)} %get-tuple-element.838), channel_id=1, source_target_pairs={{0,32},{32,64},{64,96},{96,128},{128,160},{160,192},{192,224},{224... | collective-permute-start | bytes 98312 | tf_op jit(solution)/shard_map/while/body/eval_jaxpr/ppermute | solution.py:12
  174.5 0.8 copy-start
  174.6 0.7 copy-start.5
  245.5 0.7 copy-start.6
where the time goes:
time: 248 us; the launch traced here: 247 us
  matrix products  82.3 us (33%)
  blocking collectives  70.1 us (28%)
  starting transfers between devices  45.2 us (18%)
  other arithmetic  34.9 us (14%)
  loops' own time  10.4 us (4%)
  local copies, waits for them, and re-layouts  3.63 us (1%)
    psum x1, blocking collectives, body(): square_sum = lax.psum(jnp.sum(mixed * mixed, axis=0), 'ch')  70.1 us
    ppermute x15, starting transfers between devices, shifted(): return lax.ppermute(block, axis, route)  45.2 us
    add x256, other arithmetic, add_mode(): total + scaled[:, index][:, None] * jnp.exp(-rate[:, index][:, None] * la...  29.4 us
    dot_general x32, matrix products, spectrum_of(): jnp.einsum('rkq,qm->rkm', turned_real, sin_inner, precision=level)  16.7 us
    dot_general x32, matrix products, spectrum_of(): jnp.einsum('rkq,qm->rkm', turned_imag, sin_inner, precision=level)  15.5 us
    dot_general x32, matrix products, spectrum_of(): jnp.einsum('rkq,qm->rkm', turned_real, cos_inner, precision=level)  15.5 us
    dot_general x32, matrix products, spectrum_of(): jnp.einsum('rkq,qm->rkm', turned_imag, cos_inner, precision=level)  15.5 us
    dot_general x32, matrix products, spectrum_of(): jnp.einsum('rnq,nk->rkq', cube_rows, sin_outer, precision=level)  8.38 us
  transfers between devices with their start and end apart: 15, of which 0 were waited for; matrix products, arithmetic and copies ran while one was open for 26% of the time, Pallas kernels for 0%

commit v1 on v0

v1 whole, which is shorter than its diff:
```python
import jax
import jax.numpy as jnp
from jax import lax
from jax.sharding import PartitionSpec as P

HI = lax.Precision.HIGHEST
CHUNK = 128
CTX_MODE = "gather"
CH_MODE = "butterfly"


def shifted(block, axis, distance, cyclic=False):
    size = lax.axis_size(axis)
    if cyclic:
        route = [(i, (i + distance) % size) for i in range(size)]
    else:
        route = [(i, i + distance) for i in range(size) if i + distance < size]
    return lax.ppermute(block, axis, route)


def ctx_state(block_state, rate, block_len):
    count = lax.axis_size("ctx")
    position = lax.axis_index("ctx")
    if CTX_MODE == "gather":
        every = lax.all_gather(block_state, "ctx")
        earlier = jnp.arange(count)
        gap = jnp.maximum(position - 1 - earlier, 0).astype(jnp.float32)
        weight = jnp.exp(-rate[None] * block_len * gap[:, None, None])
        weight = jnp.where((earlier < position)[:, None, None], weight, 0.0)
        return jnp.sum(weight * every, axis=0)
    total = jnp.zeros_like(block_state)
    for distance in range(1, count):
        arrived = shifted(block_state, "ctx", distance)
        total = total + jnp.exp(-rate * (block_len * (distance - 1.0))) * arrived
    return total


def ch_sum(part):
    count = lax.axis_size("ch")
    if CH_MODE == "psum":
        return lax.psum(part, "ch")
    if CH_MODE == "butterfly":
        total = part
        step = 1
        while step < count:
            route = [(i, i ^ step) for i in range(count)]
            total = total + lax.ppermute(total, "ch", route)
            step *= 2
        return total
    total = part
    for distance in range(1, count):
        total = total + shifted(part, "ch", distance, cyclic=True)
    return total


def body(query, key_branch, value_branch, residue, rate, skip, gain):
    f32 = jnp.float32
    signal = (key_branch * value_branch).astype(jnp.bfloat16)
    sig = signal.astype(f32)
    rows, block_len = sig.shape
    chunk = min(CHUNK, block_len)
    chunks = block_len // chunk
    scaled = jnp.sqrt(-jnp.expm1(-2.0 * rate)) * residue
    lag = jnp.arange(chunk, dtype=f32)
    rate3 = rate[:, :, None]

    fall = scaled[:, :, None] * jnp.exp(-rate3 * lag)
    rise = jnp.exp(rate3 * lag)
    toeplitz = jnp.einsum("cmi,cmj->cij", fall, rise, precision=HI)
    toeplitz = jnp.where(lag[:, None] >= lag[None, :], toeplitz, 0.0)
    pieces = sig.reshape(rows, chunks, chunk)
    inner = jnp.einsum("ckj,cij->cki", pieces, toeplitz, precision=HI)

    tail = jnp.exp(-rate3 * (chunk - 1.0 - lag))
    ends = jnp.einsum("ckj,cmj->ckm", pieces, tail, precision=HI)
    later = jnp.arange(chunks + 1)[:, None]
    earlier = jnp.arange(chunks)[None, :]
    steps = jnp.maximum(later - 1 - earlier, 0).astype(f32)
    carry = jnp.exp(-rate[:, :, None, None] * (chunk * steps))
    carry = jnp.where(earlier < later, carry, 0.0)
    local = jnp.einsum("cmkq,cqm->ckm", carry, ends, precision=HI)
    block_state = local[:, chunks, :]

    before = ctx_state(block_state, rate, float(block_len))
    start = jnp.arange(chunks, dtype=f32)
    entering = jnp.exp(-rate[:, None, :] * (chunk * start)[None, :, None]) * before[:, None, :]
    entering = entering + local[:, :chunks, :]
    reach = scaled[:, :, None] * jnp.exp(-rate3 * (lag + 1.0))
    outer = jnp.einsum("ckm,cmi->cki", entering, reach, precision=HI)
    conv = (inner + outer).reshape(rows, block_len)

    mixed = query.astype(f32) * (conv + skip[:, None] * sig)
    channel_total = rows * lax.axis_size("ch")
    square_sum = ch_sum(jnp.sum(mixed * mixed, axis=0))
    mean_square = square_sum / channel_total
    return (mixed / jnp.sqrt(mean_square + 1e-06)[None, :] * gain[:, None]).astype(jnp.bfloat16)


def solution(mesh):
    placed = (
        P("ch", "ctx"),
        P("ch", "ctx"),
        P("ch", "ctx"),
        P("ch", None),
        P("ch", None),
        P("ch"),
        P("ch"),
    )
    return jax.shard_map(
        body, mesh=mesh, in_specs=placed, out_specs=P("ch", "ctx"), check_vma=False
    )
```

time: 248 us -> 75.9 us (0.31)
  the two profiles are of different devices: /device:TPU:4 before, /device:TPU:2 now
where the time goes in v1:
time: 75.9 us; the launch traced here: 75.5 us
  starting transfers between devices  35.6 us (47%)
  blocking collectives  24 us (32%)
  waiting for transfers between devices  8.53 us (11%)
  matrix products  3.51 us (5%)
  other arithmetic  2.19 us (3%)
  local copies, waits for them, and re-layouts  1.38 us (2%)
    ppermute x5, starting transfers between devices, ch_sum(): total = total + lax.ppermute(total, 'ch', route)  35.6 us
    all_gather x1, blocking collectives, ctx_state(): every = lax.all_gather(block_state, 'ctx')  24 us
    ppermute x5, waiting for transfers between devices, ch_sum(): total = total + lax.ppermute(total, 'ch', route)  8.53 us
    dot_general x1, matrix products, body(): toeplitz = jnp.einsum('cmi,cmj->cij', fall, rise, precision=HI)  1.93 us
  transfers between devices with their start and end apart: 5, of which 5 were waited for; matrix products, arithmetic and copies ran while one was open for 0% of the time, Pallas kernels for 0%

profile of v1, /device:TPU:2, one launch (start us, length us, event | category | flops | bytes accessed | tf_op | source)
XLA Modules:
  0.0 75.5 jit_solution(2270165061090977619)
XLA Ops:
  0.1 0.8 %multiply_bitcast_fusion = bf16[2,8,8,128]{3,1,2,0:T(8,128)(2,1)S(1)} fusion(bf16[16,1024]{1,0:T(8,128)(2,1)} %param.8, bf16[16,1024]{1,0:T(8,128)(2,1)} %param.9), kind=kLoop, calls=%fused_computation.38 | loop fusion | flops 16384 | bytes 98304
  0.9 0.0 copy-start.3
  0.9 0.0 copy-start.4
  0.9 0.7 copy-done.3
  1.6 0.0 copy-done.4
  1.6 1.9 %convolution_select_fusion = f32[16,128,128]{2,1,0:T(8,128)S(1)} fusion(pred[128,128]{1,0:T(8,128)(4,1)S(1)} %iota_compare_fusion, f32[16,16]{1,0:T(8,128)S(1)} %copy-done.3, f32[16,16]{1,0:T(8,128)S(1)} %get-tuple-element.7, f32[16,16]{1,0:T(8,128)S(1)} %get-tuple-element.6), kind=kOutput, calls=%fused_computation | convolution fusion | flops 50692096 | bytes 1068032 | tf_op jit(solution)/shard_map/cmi,cmj->cij/dot_general | solution.py:69
  3.6 0.9 %fusion.28 = f32[16,8,128]{2,1,0:T(8,128)S(1)} fusion(bf16[16,8,128]{2,1,0:T(8,128)(2,1)S(1)} %bitcast.30, f32[16,128,128]{2,1,0:T(8,128)S(1)} %convolution_select_fusion), kind=kOutput, calls=%fused_computation.50 | convolution fusion | flops 25165824 | bytes 1146880 | tf_op jit(solution)/shard_map/ckj,cij->cki/dot_general | solution.py:72
  4.5 0.3 convolution_bitcast_fusion
  4.8 0.1 convert_multiply_fusion
  4.9 0.3 multiply_reduce_fusion
  5.2 24.0 %all-gather = f32[256,1,16]{2,1,0:T(1,128)S(1)} all-gather(f32[16,1,16]{2,1,0:T(1,128)S(1)} %slice.8), channel_id=2, replica_groups=mesh['ctx'=16,'ch'=32] {'ctx'}, dimensions={0}, use_global_device_ids=true | all-gather | bytes 17408 | tf_op jit(solution)/shard_map/all_gather | solution.py:25
  29.3 0.1 fusion
  29.4 0.0 copy-start
  29.4 0.0 copy-start.1
  29.4 0.0 copy-start.2
  29.4 0.3 convolution_add_fusion
  29.8 0.0 copy-start.5
  29.8 0.4 copy-done
  30.1 0.0 copy-done.1
  30.2 0.0 copy-done.2
  30.2 0.3 copy-done.5
  30.4 0.1 multiply_reduce_fusion.1
  30.5 3.3 %collective-permute-start = (f32[1024]{0:T(1024)S(1)}, f32[1024]{0:T(1024)S(1)}, u32[]{:S(2)}, u32[]{:S(2)}) collective-permute-start(f32[1024]{0:T(1024)S(1)} %multiply_reduce_fusion.1), channel_id=1, source_target_pairs={{0,1},{1,0},{2,3},{3,2},{4,5},{5,4},{6,7},{7,6},{8,9},{9,8},{10,11... | collective-permute-start | bytes 12296 | tf_op jit(solution)/shard_map/ppermute | solution.py:47
  33.9 2.2 %collective-permute-done = f32[1024]{0:T(1024)S(1)} collective-permute-done((f32[1024]{0:T(1024)S(1)}, f32[1024]{0:T(1024)S(1)}, u32[]{:S(2)}, u32[]{:S(2)}) %collective-permute-start) | collective-permute-done | bytes 4128 | tf_op jit(solution)/shard_map/ppermute | solution.py:47
  36.0 3.8 %collective-permute-start.1 = (f32[1024]{0:T(1024)S(1)}, f32[1024]{0:T(1024)S(1)}, u32[]{:S(2)}, u32[]{:S(2)}) collective-permute-start(f32[1024]{0:T(1024)S(1)} %add.52), channel_id=1, source_target_pairs={{0,2},{1,3},{2,0},{3,1},{4,6},{5,7},{6,4},{7,5},{8,10},{9,11},{10,... | collective-permute-start | bytes 12296 | tf_op jit(solution)/shard_map/ppermute | solution.py:47
  39.9 1.7 %collective-permute-done.1 = f32[1024]{0:T(1024)S(1)} collective-permute-done((f32[1024]{0:T(1024)S(1)}, f32[1024]{0:T(1024)S(1)}, u32[]{:S(2)}, u32[]{:S(2)}) %collective-permute-start.1) | collective-permute-done | bytes 4128 | tf_op jit(solution)/shard_map/ppermute | solution.py:47
  41.5 5.2 %collective-permute-start.2 = (f32[1024]{0:T(1024)S(1)}, f32[1024]{0:T(1024)S(1)}, u32[]{:S(2)}, u32[]{:S(2)}) collective-permute-start(f32[1024]{0:T(1024)S(1)} %add.53), channel_id=1, source_target_pairs={{0,4},{1,5},{2,6},{3,7},{4,0},{5,1},{6,2},{7,3},{8,12},{9,13},{10,... | collective-permute-start | bytes 12296 | tf_op jit(solution)/shard_map/ppermute | solution.py:47
  46.7 1.6 %collective-permute-done.2 = f32[1024]{0:T(1024)S(1)} collective-permute-done((f32[1024]{0:T(1024)S(1)}, f32[1024]{0:T(1024)S(1)}, u32[]{:S(2)}, u32[]{:S(2)}) %collective-permute-start.2) | collective-permute-done | bytes 4128 | tf_op jit(solution)/shard_map/ppermute | solution.py:47
  48.3 9.1 %collective-permute-start.3 = (f32[1024]{0:T(1024)S(1)}, f32[1024]{0:T(1024)S(1)}, u32[]{:S(2)}, u32[]{:S(2)}) collective-permute-start(f32[1024]{0:T(1024)S(1)} %add.54), channel_id=1, source_target_pairs={{0,8},{1,9},{2,10},{3,11},{4,12},{5,13},{6,14},{7,15},{8,0},{9,1},... | collective-permute-start | bytes 12296 | tf_op jit(solution)/shard_map/ppermute | solution.py:47
  57.4 1.6 %collective-permute-done.3 = f32[1024]{0:T(1024)S(1)} collective-permute-done((f32[1024]{0:T(1024)S(1)}, f32[1024]{0:T(1024)S(1)}, u32[]{:S(2)}, u32[]{:S(2)}) %collective-permute-start.3) | collective-permute-done | bytes 4128 | tf_op jit(solution)/shard_map/ppermute | solution.py:47
  59.0 0.0 copy-start.6
  59.0 14.2 %collective-permute-start.4 = (f32[1024]{0:T(1024)S(1)}, f32[1024]{0:T(1024)S(1)}, u32[]{:S(2)}, u32[]{:S(2)}) collective-permute-start(f32[1024]{0:T(1024)S(1)} %add.55), channel_id=1, source_target_pairs={{0,16},{1,17},{2,18},{3,19},{4,20},{5,21},{6,22},{7,23},{8,24},{9,... | collective-permute-start | bytes 12296 | tf_op jit(solution)/shard_map/ppermute | solution.py:47
  73.2 1.6 %collective-permute-done.4 = f32[1024]{0:T(1024)S(1)} collective-permute-done((f32[1024]{0:T(1024)S(1)}, f32[1024]{0:T(1024)S(1)}, u32[]{:S(2)}, u32[]{:S(2)}) %collective-permute-start.4) | collective-permute-done | bytes 4128 | tf_op jit(solution)/shard_map/ppermute | solution.py:47
  74.8 0.0 copy-done.6
  74.8 0.7 multiply_convert_fusion
  (16 shorter events, 0.1 us)
Async XLA Ops:
  0.9 0.7 copy-start.3
  0.9 0.7 copy-start.4
  29.4 0.8 %copy-start = (bf16[16,1024]{1,0:T(8,128)(2,1)S(1)}, bf16[16,1024]{1,0:T(8,128)(2,1)}, u32[]{:S(2)}) copy-start(bf16[16,1024]{1,0:T(8,128)(2,1)} %param.8) | copy-start | bytes 98308
  29.4 0.8 %copy-start.1 = (bf16[16,1024]{1,0:T(8,128)(2,1)S(1)}, bf16[16,1024]{1,0:T(8,128)(2,1)}, u32[]{:S(2)}) copy-start(bf16[16,1024]{1,0:T(8,128)(2,1)} %param.9) | copy-start | bytes 98308
  29.4 0.8 %copy-start.2 = (bf16[16,1024]{1,0:T(8,128)(2,1)S(1)}, bf16[16,1024]{1,0:T(8,128)(2,1)}, u32[]{:S(2)}) copy-start(bf16[16,1024]{1,0:T(8,128)(2,1)} %param.7) | copy-start | bytes 98308
  29.8 0.7 copy-start.5
  30.5 5.5 %collective-permute-start = (f32[1024]{0:T(1024)S(1)}, f32[1024]{0:T(1024)S(1)}, u32[]{:S(2)}, u32[]{:S(2)}) collective-permute-start(f32[1024]{0:T(1024)S(1)} %multiply_reduce_fusion.1), channel_id=1, source_target_pairs={{0,1},{1,0},{2,3},{3,2},{4,5},{5,4},{6,7},{7,6},{8,9},{9,8},{10,11... | collective-permute-start | bytes 12296 | tf_op jit(solution)/shard_map/ppermute | solution.py:47
  36.0 5.5 %collective-permute-start.1 = (f32[1024]{0:T(1024)S(1)}, f32[1024]{0:T(1024)S(1)}, u32[]{:S(2)}, u32[]{:S(2)}) collective-permute-start(f32[1024]{0:T(1024)S(1)} %add.52), channel_id=1, source_target_pairs={{0,2},{1,3},{2,0},{3,1},{4,6},{5,7},{6,4},{7,5},{8,10},{9,11},{10,... | collective-permute-start | bytes 12296 | tf_op jit(solution)/shard_map/ppermute | solution.py:47
  41.5 6.7 %collective-permute-start.2 = (f32[1024]{0:T(1024)S(1)}, f32[1024]{0:T(1024)S(1)}, u32[]{:S(2)}, u32[]{:S(2)}) collective-permute-start(f32[1024]{0:T(1024)S(1)} %add.53), channel_id=1, source_target_pairs={{0,4},{1,5},{2,6},{3,7},{4,0},{5,1},{6,2},{7,3},{8,12},{9,13},{10,... | collective-permute-start | bytes 12296 | tf_op jit(solution)/shard_map/ppermute | solution.py:47
  48.3 10.7 %collective-permute-start.3 = (f32[1024]{0:T(1024)S(1)}, f32[1024]{0:T(1024)S(1)}, u32[]{:S(2)}, u32[]{:S(2)}) collective-permute-start(f32[1024]{0:T(1024)S(1)} %add.54), channel_id=1, source_target_pairs={{0,8},{1,9},{2,10},{3,11},{4,12},{5,13},{6,14},{7,15},{8,0},{9,1},... | collective-permute-start | bytes 12296 | tf_op jit(solution)/shard_map/ppermute | solution.py:47
  59.0 15.8 %copy-start.6 = (f32[16]{0:T(128)S(1)}, f32[16]{0:T(128)}, u32[]{:S(2)}) copy-start(f32[16]{0:T(128)} %param.13) | copy-start | bytes 196
  59.0 15.8 %collective-permute-start.4 = (f32[1024]{0:T(1024)S(1)}, f32[1024]{0:T(1024)S(1)}, u32[]{:S(2)}, u32[]{:S(2)}) collective-permute-start(f32[1024]{0:T(1024)S(1)} %add.55), channel_id=1, source_target_pairs={{0,16},{1,17},{2,18},{3,19},{4,20},{5,21},{6,22},{7,23},{8,24},{9,... | collective-permute-start | bytes 12296 | tf_op jit(solution)/shard_map/ppermute | solution.py:47

commit v2 on v1

--- a/solution.py
+++ b/solution.py
@@ -5,8 +5,8 @@
 
 HI = lax.Precision.HIGHEST
 CHUNK = 128
-CTX_MODE = "gather"
-CH_MODE = "butterfly"
+CTX_MODE = "a2a"
+CH_MODE = "a2a"
 
 
 def shifted(block, axis, distance, cyclic=False):
@@ -18,11 +18,20 @@
     return lax.ppermute(block, axis, route)
 
 
+def everyone(block, axis):
+    count = lax.axis_size(axis)
+    copies = jnp.broadcast_to(block[None], (count,) + block.shape)
+    return lax.all_to_all(copies, axis, 0, 0, tiled=True)
+
+
 def ctx_state(block_state, rate, block_len):
     count = lax.axis_size("ctx")
     position = lax.axis_index("ctx")
-    if CTX_MODE == "gather":
-        every = lax.all_gather(block_state, "ctx")
+    if CTX_MODE in ("gather", "a2a"):
+        if CTX_MODE == "gather":
+            every = lax.all_gather(block_state, "ctx")
+        else:
+            every = everyone(block_state, "ctx")
         earlier = jnp.arange(count)
         gap = jnp.maximum(position - 1 - earlier, 0).astype(jnp.float32)
         weight = jnp.exp(-rate[None] * block_len * gap[:, None, None])
@@ -39,6 +48,8 @@
     count = lax.axis_size("ch")
     if CH_MODE == "psum":
         return lax.psum(part, "ch")
+    if CH_MODE == "a2a":
+        return jnp.sum(everyone(part, "ch"), axis=0)
     if CH_MODE == "butterfly":
         total = part
         step = 1

time: 75.9 us -> 53.9 us (0.71)
  starting transfers between devices: 35.6 us -> 6.14 us
  blocking collectives: 24 us -> 32.8 us
  waiting for transfers between devices: 8.53 us -> 4.64 us
  local copies, waits for them, and re-layouts: 1.38 us -> 3.34 us
  other arithmetic: 2.19 us -> 2.96 us
    ppermute x5 -> x0, starting transfers between devices: 35.6 us -> none  [ch_sum(): total = total + lax.ppermute(total, 'ch', route)]
    all_to_all x0 -> x1, blocking collectives: none -> 32.8 us  [everyone(): return lax.all_to_all(copies, axis, 0, 0, tiled=True)]
    all_gather x1 -> x0, blocking collectives: 24 us -> none  [ctx_state(): every = lax.all_gather(block_state, 'ctx')]
    ppermute x5 -> x0, waiting for transfers between devices: 8.53 us -> none  [ch_sum(): total = total + lax.ppermute(total, 'ch', route)]
    all_to_all x0 -> x1, starting transfers between devices: none -> 6.14 us  [everyone(): return lax.all_to_all(copies, axis, 0, 0, tiled=True)]
    all_to_all x0 -> x1, waiting for transfers between devices: none -> 4.64 us  [everyone(): return lax.all_to_all(copies, axis, 0, 0, tiled=True)]
    unnamed x15 -> x17, local copies, waits for them, and re-layouts: 1.37 us -> 2.74 us
  transfers between devices with their start and end apart: 5 -> 1, of which waited for: 5 -> 1; matrix products, arithmetic and copies ran while one was open for 0% -> 5% of each run, Pallas kernels for 0% -> 0%
where the time goes in v2:
time: 53.9 us; the launch traced here: 53.5 us
  blocking collectives  32.8 us (61%)
  starting transfers between devices  6.14 us (11%)
  waiting for transfers between devices  4.64 us (9%)
  matrix products  3.49 us (6%)
  local copies, waits for them, and re-layouts  3.34 us (6%)
  other arithmetic  2.96 us (5%)
    all_to_all x1, blocking collectives, everyone(): return lax.all_to_all(copies, axis, 0, 0, tiled=True)  32.8 us
    all_to_all x1, starting transfers between devices, everyone(): return lax.all_to_all(copies, axis, 0, 0, tiled=True)  6.14 us
    all_to_all x1, waiting for transfers between devices, everyone(): return lax.all_to_all(copies, axis, 0, 0, tiled=True)  4.64 us
    unnamed x17, local copies, waits for them, and re-layouts  2.74 us
    dot_general x1, matrix products, body(): toeplitz = jnp.einsum('cmi,cmj->cij', fall, rise, precision=HI)  1.93 us
  transfers between devices with their start and end apart: 1, of which 1 were waited for; matrix products, arithmetic and copies ran while one was open for 5% of the time, Pallas kernels for 0%

profile of v2, /device:TPU:2, one launch (start us, length us, event | category | flops | bytes accessed | tf_op | source)
XLA Modules:
  0.0 53.5 jit_solution(748582478771587437)
XLA Ops:
  0.0 0.8 %multiply_bitcast_fusion = bf16[2,8,8,128]{3,1,2,0:T(8,128)(2,1)S(1)} fusion(bf16[16,1024]{1,0:T(8,128)(2,1)} %param.8, bf16[16,1024]{1,0:T(8,128)(2,1)} %param.9), kind=kLoop, calls=%fused_computation.37 | loop fusion | flops 16384 | bytes 98304
  0.8 0.0 copy-start.4
  0.8 0.0 copy-start.3
  0.8 0.1 convert_multiply_fusion
  0.9 0.6 %copy-done.4 = f32[16,16]{1,0:T(8,128)S(1)} copy-done((f32[16,16]{1,0:T(8,128)S(1)}, f32[16,16]{1,0:T(8,128)}, u32[]{:S(2)}) %copy-start.4) | copy-done | bytes 1048
  1.5 0.0 copy-done.3
  1.5 0.3 convolution_bitcast_fusion
  1.9 0.3 multiply_reduce_fusion
  2.2 0.7 %reshape.85 = f32[16,1,256]{2,1,0:T(1,128)} reshape(f32[16,16,16]{2,1,0:T(8,128)S(1)} %broadcast_in_dim.41) | data formatting | bytes 32768
  2.9 6.1 %all-to-all-start = ((f32[16,1,256]{2,1,0:T(1,128)}), f32[16,1,256]{2,1,0:T(1,128)S(1)}, u32[]{:S(2)}, u32[]{:S(2)}) async-start(f32[16,1,256]{2,1,0:T(1,128)} %reshape.85), calls=%async_computation | async-start | bytes 32768 | tf_op jit(solution)/shard_map/all_to_all | solution.py:24
  9.1 1.9 %convolution_select_fusion = f32[16,128,128]{2,1,0:T(8,128)S(1)} fusion(pred[128,128]{1,0:T(8,128)(4,1)S(1)} %iota_compare_fusion, f32[16,16]{1,0:T(8,128)S(1)} %copy-done.3, f32[16,16]{1,0:T(8,128)S(1)} %get-tuple-element.7, f32[16,16]{1,0:T(8,128)S(1)} %get-tuple-element.6), kind=kOutput, calls=%fused_computation | convolution fusion | flops 50692096 | bytes 1068032 | tf_op jit(solution)/shard_map/cmi,cmj->cij/dot_general | solution.py:80
  11.1 0.9 %fusion.27 = f32[16,8,128]{2,1,0:T(8,128)S(1)} fusion(bf16[16,8,128]{2,1,0:T(8,128)(2,1)S(1)} %bitcast.26, f32[16,128,128]{2,1,0:T(8,128)S(1)} %convolution_select_fusion), kind=kOutput, calls=%fused_computation.49 | convolution fusion | flops 25165824 | bytes 1146880 | tf_op jit(solution)/shard_map/ckj,cij->cki/dot_general | solution.py:83
  12.0 4.6 %all-to-all-done = f32[16,1,256]{2,1,0:T(1,128)S(1)} async-done(((f32[16,1,256]{2,1,0:T(1,128)}), f32[16,1,256]{2,1,0:T(1,128)S(1)}, u32[]{:S(2)}, u32[]{:S(2)}) %all-to-all-start) | async-done | bytes 16416 | tf_op jit(solution)/shard_map/all_to_all | solution.py:24
  16.7 0.5 broadcast.86
  17.2 0.7 %reduce.3 = f32[16,256]{1,0:T(8,128)S(1)} reduce(f32[16,1,256]{2,1,0:T(1,128)S(1)} %all-to-all-done, f32[]{:T(128)} %broadcast.86), dimensions={1}, to_apply=%all_to_all.7.reduce_sub_computation | reduce | bytes 32772 | tf_op jit(solution)/shard_map/all_to_all | solution.py:24
  17.9 0.1 reshape.86
  18.0 0.1 multiply_reduce_fusion.1
  18.1 0.0 copy-start
  18.1 0.0 copy-start.1
  18.1 0.0 copy-start.2
  18.1 0.3 convolution_add_fusion
  18.5 0.0 copy-start.5
  18.5 0.4 copy-done
  18.8 0.0 copy-done.1
  18.9 0.0 copy-done.2
  18.9 0.3 copy-done.5
  19.1 0.1 multiply_reduce_fusion.2
  19.2 0.1 broadcast_in_dim.42
  19.3 32.8 %all_to_all.11 = f32[32,1,1024]{2,1,0:T(1,128)S(1)} all-to-all(f32[32,1,1024]{2,1,0:T(1,128)S(1)} %broadcast_in_dim.42), channel_id=1, replica_groups=mesh['ctx'=16,'ch'=32] {'ch'}, dimensions={0} | all-to-all | bytes 262144 | tf_op jit(solution)/shard_map/all_to_all | solution.py:24
  52.1 0.1 reduce_sum.29
  52.2 0.0 copy-start.6
  52.2 0.6 %copy-done.6 = f32[16]{0:T(128)S(1)} copy-done((f32[16]{0:T(128)S(1)}, f32[16]{0:T(128)}, u32[]{:S(2)}) %copy-start.6) | copy-done | bytes 88
  52.8 0.7 %multiply_convert_fusion = bf16[16,1024]{1,0:T(8,128)(2,1)} fusion(f32[16]{0:T(128)S(1)} %copy-done.6, f32[1024]{0:T(1024)S(1)} %add_sqrt_fusion, bf16[16,1024]{1,0:T(8,128)(2,1)S(1)} %copy-done, bf16[16,1024]{1,0:T(8,128)(2,1)S(1)} %copy-done.1, f32[16]{0:T(128)S(1)} %copy-done.5, f32[2,8,8,128]{3,2,1,0:T(8,128)S(1)} %bitcast.22, ...), kind=kLoop, calls=%fused_computation.20 | loop fusion | flops 147456 | bytes 200832 | tf_op jit(solution)/shard_map/convert_element_type | solution.py:107
  (13 shorter events, 0.1 us)
Async XLA Ops:
  0.8 0.7 %copy-start.4 = (f32[16,16]{1,0:T(8,128)S(1)}, f32[16,16]{1,0:T(8,128)}, u32[]{:S(2)}) copy-start(f32[16,16]{1,0:T(8,128)} %param.10) | copy-start | bytes 3076
  0.8 0.7 %copy-start.3 = (f32[16,16]{1,0:T(8,128)S(1)}, f32[16,16]{1,0:T(8,128)}, u32[]{:S(2)}) copy-start(f32[16,16]{1,0:T(8,128)} %param.11) | copy-start | bytes 3076
  2.9 13.7 %all-to-all-start = ((f32[16,1,256]{2,1,0:T(1,128)}), f32[16,1,256]{2,1,0:T(1,128)S(1)}, u32[]{:S(2)}, u32[]{:S(2)}) async-start(f32[16,1,256]{2,1,0:T(1,128)} %reshape.85), calls=%async_computation | async-start | bytes 32768 | tf_op jit(solution)/shard_map/all_to_all | solution.py:24
  18.1 0.8 %copy-start = (bf16[16,1024]{1,0:T(8,128)(2,1)S(1)}, bf16[16,1024]{1,0:T(8,128)(2,1)}, u32[]{:S(2)}) copy-start(bf16[16,1024]{1,0:T(8,128)(2,1)} %param.8) | copy-start | bytes 98308
  18.1 0.8 %copy-start.1 = (bf16[16,1024]{1,0:T(8,128)(2,1)S(1)}, bf16[16,1024]{1,0:T(8,128)(2,1)}, u32[]{:S(2)}) copy-start(bf16[16,1024]{1,0:T(8,128)(2,1)} %param.9) | copy-start | bytes 98308
  18.1 0.8 %copy-start.2 = (bf16[16,1024]{1,0:T(8,128)(2,1)S(1)}, bf16[16,1024]{1,0:T(8,128)(2,1)}, u32[]{:S(2)}) copy-start(bf16[16,1024]{1,0:T(8,128)(2,1)} %param.7) | copy-start | bytes 98308
  18.5 0.7 %copy-start.5 = (f32[16]{0:T(128)S(1)}, f32[16]{0:T(128)}, u32[]{:S(2)}) copy-start(f32[16]{0:T(128)} %param.12) | copy-start | bytes 196
  52.2 0.7 %copy-start.6 = (f32[16]{0:T(128)S(1)}, f32[16]{0:T(128)}, u32[]{:S(2)}) copy-start(f32[16]{0:T(128)} %param.13) | copy-start | bytes 196

commit v3 on v2

--- a/solution.py
+++ b/solution.py
@@ -7,6 +7,8 @@
 CHUNK = 128
 CTX_MODE = "a2a"
 CH_MODE = "a2a"
+FLAT_STATE = True
+CH_TYPE = jnp.bfloat16
 
 
 def shifted(block, axis, distance, cyclic=False):
@@ -30,6 +32,13 @@
     if CTX_MODE in ("gather", "a2a"):
         if CTX_MODE == "gather":
             every = lax.all_gather(block_state, "ctx")
+        elif FLAT_STATE:
+            rows, modes = block_state.shape
+            every = everyone(block_state.reshape(rows * modes), "ctx")
+            gap = jnp.maximum(position - 1 - jnp.arange(count), 0).astype(jnp.float32)
+            weight = jnp.exp(-rate.reshape(1, rows * modes) * block_len * gap[:, None])
+            weight = jnp.where((jnp.arange(count) < position)[:, None], weight, 0.0)
+            return jnp.sum(weight * every, axis=0).reshape(rows, modes)
         else:
             every = everyone(block_state, "ctx")
         earlier = jnp.arange(count)
@@ -49,7 +58,8 @@
     if CH_MODE == "psum":
         return lax.psum(part, "ch")
     if CH_MODE == "a2a":
-        return jnp.sum(everyone(part, "ch"), axis=0)
+        every = everyone(part.astype(CH_TYPE), "ch")
+        return jnp.sum(every.astype(jnp.float32), axis=0)
     if CH_MODE == "butterfly":
         total = part
         step = 1

time: 53.9 us -> 51.4 us (0.954)
  blocking collectives: 32.8 us -> 30 us
    all_to_all x1, blocking collectives: 32.8 us -> 30 us  [everyone(): return lax.all_to_all(copies, axis, 0, 0, tiled=True)]
    broadcast_in_dim x2 -> x4, local copies, waits for them, and re-layouts: 0.08 us -> 1.29 us  [everyone(): copies = jnp.broadcast_to(block[None], (count,) + block.shape)]
    broadcast_in_dim x0 -> x1, other arithmetic: none -> 1 us  [everyone(): copies = jnp.broadcast_to(block[None], (count,) + block.shape)]
    unnamed x17, local copies, waits for them, and re-layouts: 2.74 us -> 2.01 us
    all_to_all x1 -> x0, other arithmetic: 0.68 us -> none  [everyone(): return lax.all_to_all(copies, axis, 0, 0, tiled=True)]
  transfers between devices with their start and end apart: 1 -> 1, of which waited for: 1 -> 1; matrix products, arithmetic and copies ran while one was open for 5% -> 6% of each run, Pallas kernels for 0% -> 0%
where the time goes in v3:
time: 51.4 us; the launch traced here: 51 us
  blocking collectives  30 us (58%)
  starting transfers between devices  6.14 us (12%)
  waiting for transfers between devices  4.56 us (9%)
  matrix products  3.49 us (7%)
  local copies, waits for them, and re-layouts  3.48 us (7%)
  other arithmetic  3.21 us (6%)
    all_to_all x1, blocking collectives, everyone(): return lax.all_to_all(copies, axis, 0, 0, tiled=True)  30 us
    all_to_all x1, starting transfers between devices, everyone(): return lax.all_to_all(copies, axis, 0, 0, tiled=True)  6.14 us
    all_to_all x1, waiting for transfers between devices, everyone(): return lax.all_to_all(copies, axis, 0, 0, tiled=True)  4.56 us
    unnamed x17, local copies, waits for them, and re-layouts  2.01 us
    dot_general x1, matrix products, body(): toeplitz = jnp.einsum('cmi,cmj->cij', fall, rise, precision=HI)  1.93 us
    broadcast_in_dim x4, local copies, waits for them, and re-layouts, everyone(): copies = jnp.broadcast_to(block[None], (count,) + block.shape)  1.29 us
  transfers between devices with their start and end apart: 1, of which 1 were waited for; matrix products, arithmetic and copies ran while one was open for 6% of the time, Pallas kernels for 0%

profile of v3, /device:TPU:2, one launch (start us, length us, event | category | flops | bytes accessed | tf_op | source)
XLA Modules:
  0.0 51.0 jit_solution(10849985736955858829)
XLA Ops:
  0.0 0.8 %multiply_bitcast_fusion = bf16[2,8,8,128]{3,1,2,0:T(8,128)(2,1)S(1)} fusion(bf16[16,1024]{1,0:T(8,128)(2,1)} %param.8, bf16[16,1024]{1,0:T(8,128)(2,1)} %param.9), kind=kLoop, calls=%fused_computation.39 | loop fusion | flops 16384 | bytes 98304
  0.8 0.0 copy-start.4
  0.8 0.0 copy-start.3
  0.8 0.1 convert_multiply_fusion
  0.9 0.6 %copy-done.4 = f32[16,16]{1,0:T(8,128)S(1)} copy-done((f32[16,16]{1,0:T(8,128)S(1)}, f32[16,16]{1,0:T(8,128)}, u32[]{:S(2)}) %copy-start.4) | copy-done | bytes 1048
  1.5 0.0 copy-done.3
  1.5 0.3 convolution_bitcast_fusion
  1.9 0.3 multiply_reduce_fusion
  2.2 0.1 broadcast_in_dim.40
  2.3 0.6 %broadcast_in_dim.41 = f32[16,1,256]{2,1,0:T(1,128)} broadcast(f32[256]{0:T(256)S(1)} %broadcast_in_dim.40), dimensions={2} | broadcast | bytes 17408 | tf_op jit(solution)/shard_map/broadcast_in_dim | solution.py:25
  2.9 6.1 %all-to-all-start = ((f32[16,1,256]{2,1,0:T(1,128)}), f32[16,1,256]{2,1,0:T(1,128)S(1)}, u32[]{:S(2)}, u32[]{:S(2)}) async-start(f32[16,1,256]{2,1,0:T(1,128)} %broadcast_in_dim.41), calls=%async_computation | async-start | bytes 32768 | tf_op jit(solution)/shard_map/all_to_all | solution.py:26
  9.1 1.9 %convolution_select_fusion = f32[16,128,128]{2,1,0:T(8,128)S(1)} fusion(pred[128,128]{1,0:T(8,128)(4,1)S(1)} %iota_compare_fusion, f32[16,16]{1,0:T(8,128)S(1)} %copy-done.3, f32[16,16]{1,0:T(8,128)S(1)} %get-tuple-element.7, f32[16,16]{1,0:T(8,128)S(1)} %get-tuple-element.6), kind=kOutput, calls=%fused_computation | convolution fusion | flops 50692096 | bytes 1068032 | tf_op jit(solution)/shard_map/cmi,cmj->cij/dot_general | solution.py:90
  11.1 0.9 %fusion.28 = f32[16,8,128]{2,1,0:T(8,128)S(1)} fusion(bf16[16,8,128]{2,1,0:T(8,128)(2,1)S(1)} %bitcast.29, f32[16,128,128]{2,1,0:T(8,128)S(1)} %convolution_select_fusion), kind=kOutput, calls=%fused_computation.52 | convolution fusion | flops 25165824 | bytes 1146880 | tf_op jit(solution)/shard_map/ckj,cij->cki/dot_general | solution.py:93
  12.0 0.1 mul.197
  12.1 4.6 %all-to-all-done = f32[16,1,256]{2,1,0:T(1,128)S(1)} async-done(((f32[16,1,256]{2,1,0:T(1,128)}), f32[16,1,256]{2,1,0:T(1,128)S(1)}, u32[]{:S(2)}, u32[]{:S(2)}) %all-to-all-start) | async-done | bytes 16416 | tf_op jit(solution)/shard_map/all_to_all | solution.py:26
  16.6 0.1 fusion.27
  16.7 0.1 mul.209
  16.8 0.0 copy-start
  16.8 0.0 copy-start.1
  16.8 0.0 copy-start.2
  16.8 0.3 convolution_add_fusion
  17.2 0.0 copy-start.5
  17.2 0.4 copy-done
  17.6 0.0 copy-done.1
  17.6 0.0 copy-done.2
  17.6 0.2 copy-done.5
  17.9 0.1 multiply_reduce_fusion.1
  18.0 0.1 broadcast_in_dim.42
  18.0 0.5 %broadcast.98 = bf16[]{:T(256)} broadcast(bf16[]{:T(256)} %constant.71), dimensions={} | broadcast | bytes 4 | tf_op jit(solution)/shard_map/broadcast_in_dim | solution.py:25
  18.5 1.0 %reduce.7 = bf16[32,1024]{1,0:T(8,128)(2,1)S(1)} reduce(bf16[32,1,1024]{2,1,0:T(2,128)(2,1)S(1)} %broadcast_in_dim.42, bf16[]{:T(256)} %broadcast.98), dimensions={1}, to_apply=%broadcast_in_dim.42.reduce_sub_computation | reduce | bytes 131074 | tf_op jit(solution)/shard_map/broadcast_in_dim | solution.py:25
  19.6 30.0 %all_to_all.15 = bf16[32,2,512]{2,1,0:T(2,128)(2,1)S(1)} all-to-all(bf16[32,2,512]{2,1,0:T(2,128)(2,1)S(1)} %reshape.113), channel_id=1, replica_groups=mesh['ctx'=16,'ch'=32] {'ch'}, dimensions={0} | all-to-all | bytes 131072 | tf_op jit(solution)/shard_map/all_to_all | solution.py:26
  49.6 0.1 reshape.114
  49.7 0.0 copy-start.6
  49.7 0.6 %copy-done.6 = f32[16]{0:T(128)S(1)} copy-done((f32[16]{0:T(128)S(1)}, f32[16]{0:T(128)}, u32[]{:S(2)}) %copy-start.6) | copy-done | bytes 88
  50.3 0.7 %multiply_convert_fusion = bf16[16,1024]{1,0:T(8,128)(2,1)} fusion(f32[16]{0:T(128)S(1)} %copy-done.6, f32[1024]{0:T(1024)S(1)} %add_sqrt_fusion, bf16[16,1024]{1,0:T(8,128)(2,1)S(1)} %copy-done, bf16[16,1024]{1,0:T(8,128)(2,1)S(1)} %copy-done.1, f32[16]{0:T(128)S(1)} %copy-done.5, f32[2,8,8,128]{3,2,1,0:T(8,128)S(1)} %bitcast.25, ...), kind=kLoop, calls=%fused_computation.20 | loop fusion | flops 147456 | bytes 200832 | tf_op jit(solution)/shard_map/convert_element_type | solution.py:117
  (14 shorter events, 0.2 us)
Async XLA Ops:
  0.8 0.7 %copy-start.4 = (f32[16,16]{1,0:T(8,128)S(1)}, f32[16,16]{1,0:T(8,128)}, u32[]{:S(2)}) copy-start(f32[16,16]{1,0:T(8,128)} %param.10) | copy-start | bytes 3076
  0.8 0.7 %copy-start.3 = (f32[16,16]{1,0:T(8,128)S(1)}, f32[16,16]{1,0:T(8,128)}, u32[]{:S(2)}) copy-start(f32[16,16]{1,0:T(8,128)} %param.11) | copy-start | bytes 3076
  2.9 13.7 %all-to-all-start = ((f32[16,1,256]{2,1,0:T(1,128)}), f32[16,1,256]{2,1,0:T(1,128)S(1)}, u32[]{:S(2)}, u32[]{:S(2)}) async-start(f32[16,1,256]{2,1,0:T(1,128)} %broadcast_in_dim.41), calls=%async_computation | async-start | bytes 32768 | tf_op jit(solution)/shard_map/all_to_all | solution.py:26
  16.8 0.8 %copy-start = (bf16[16,1024]{1,0:T(8,128)(2,1)S(1)}, bf16[16,1024]{1,0:T(8,128)(2,1)}, u32[]{:S(2)}) copy-start(bf16[16,1024]{1,0:T(8,128)(2,1)} %param.8) | copy-start | bytes 98308
  16.8 0.8 %copy-start.1 = (bf16[16,1024]{1,0:T(8,128)(2,1)S(1)}, bf16[16,1024]{1,0:T(8,128)(2,1)}, u32[]{:S(2)}) copy-start(bf16[16,1024]{1,0:T(8,128)(2,1)} %param.9) | copy-start | bytes 98308
  16.8 0.8 %copy-start.2 = (bf16[16,1024]{1,0:T(8,128)(2,1)S(1)}, bf16[16,1024]{1,0:T(8,128)(2,1)}, u32[]{:S(2)}) copy-start(bf16[16,1024]{1,0:T(8,128)(2,1)} %param.7) | copy-start | bytes 98308
  17.2 0.7 %copy-start.5 = (f32[16]{0:T(128)S(1)}, f32[16]{0:T(128)}, u32[]{:S(2)}) copy-start(f32[16]{0:T(128)} %param.12) | copy-start | bytes 196
  49.7 0.7 %copy-start.6 = (f32[16]{0:T(128)S(1)}, f32[16]{0:T(128)}, u32[]{:S(2)}) copy-start(f32[16]{0:T(128)} %param.13) | copy-start | bytes 196

commit v4 on v3

--- a/solution.py
+++ b/solution.py
@@ -34,7 +34,9 @@
             every = lax.all_gather(block_state, "ctx")
         elif FLAT_STATE:
             rows, modes = block_state.shape
-            every = everyone(block_state.reshape(rows * modes), "ctx")
+            shape = (-1, 128) if (rows * modes) % 128 == 0 else (rows * modes,)
+            every = everyone(block_state.reshape(shape), "ctx")
+            every = every.reshape(count, rows * modes)
             gap = jnp.maximum(position - 1 - jnp.arange(count), 0).astype(jnp.float32)
             weight = jnp.exp(-rate.reshape(1, rows * modes) * block_len * gap[:, None])
             weight = jnp.where((jnp.arange(count) < position)[:, None], weight, 0.0)
@@ -58,6 +60,9 @@
     if CH_MODE == "psum":
         return lax.psum(part, "ch")
     if CH_MODE == "a2a":
+        if part.shape[0] % 128 == 0:
+            every = everyone(part.astype(CH_TYPE).reshape(-1, 128), "ch")
+            return jnp.sum(every.astype(jnp.float32), axis=0).reshape(part.shape)
         every = everyone(part.astype(CH_TYPE), "ch")
         return jnp.sum(every.astype(jnp.float32), axis=0)
     if CH_MODE == "butterfly":

time: 51.4 us -> 49.7 us (0.967)
  other arithmetic: 3.21 us -> 2.22 us
  local copies, waits for them, and re-layouts: 3.48 us -> 2.82 us
    broadcast_in_dim x1 -> x0, other arithmetic: 1 us -> none  [everyone(): copies = jnp.broadcast_to(block[None], (count,) + block.shape)]
    broadcast_in_dim x4 -> x3, local copies, waits for them, and re-layouts: 1.29 us -> 0.71 us  [everyone(): copies = jnp.broadcast_to(block[None], (count,) + block.shape)]
    unnamed x17 -> x15, local copies, waits for them, and re-layouts: 2.01 us -> 1.93 us
where the time goes in v4:
time: 49.7 us; the launch traced here: 49.3 us
  blocking collectives  30 us (60%)
  starting transfers between devices  6.14 us (12%)
  waiting for transfers between devices  4.56 us (9%)
  matrix products  3.49 us (7%)
  local copies, waits for them, and re-layouts  2.82 us (6%)
  other arithmetic  2.22 us (4%)
    all_to_all x1, blocking collectives, everyone(): return lax.all_to_all(copies, axis, 0, 0, tiled=True)  30 us
    all_to_all x1, starting transfers between devices, everyone(): return lax.all_to_all(copies, axis, 0, 0, tiled=True)  6.14 us
    all_to_all x1, waiting for transfers between devices, everyone(): return lax.all_to_all(copies, axis, 0, 0, tiled=True)  4.56 us
    dot_general x1, matrix products, body(): toeplitz = jnp.einsum('cmi,cmj->cij', fall, rise, precision=HI)  1.93 us
    unnamed x15, local copies, waits for them, and re-layouts  1.93 us
  transfers between devices with their start and end apart: 1, of which 1 were waited for; matrix products, arithmetic and copies ran while one was open for 6% of the time, Pallas kernels for 0%

profile of v4, /device:TPU:2, one launch (start us, length us, event | category | flops | bytes accessed | tf_op | source)
XLA Modules:
  0.0 49.3 jit_solution(1387525581573250849)
XLA Ops:
  0.0 0.8 %multiply_bitcast_fusion = bf16[2,8,8,128]{3,1,2,0:T(8,128)(2,1)S(1)} fusion(bf16[16,1024]{1,0:T(8,128)(2,1)} %param.8, bf16[16,1024]{1,0:T(8,128)(2,1)} %param.9), kind=kLoop, calls=%fused_computation.38 | loop fusion | flops 16384 | bytes 98304
  0.8 0.0 copy-start.4
  0.8 0.0 copy-start.3
  0.8 0.1 convert_multiply_fusion
  0.9 0.6 %copy-done.4 = f32[16,16]{1,0:T(8,128)S(1)} copy-done((f32[16,16]{1,0:T(8,128)S(1)}, f32[16,16]{1,0:T(8,128)}, u32[]{:S(2)}) %copy-start.4) | copy-done | bytes 1048
  1.5 0.0 copy-done.3
  1.5 0.3 convolution_bitcast_fusion
  1.9 0.3 multiply_reduce_fusion
  2.2 0.1 broadcast_in_dim.40
  2.3 0.6 %broadcast_in_dim.41 = f32[16,2,128]{2,1,0:T(2,128)} broadcast(f32[2,128]{1,0:T(2,128)S(1)} %broadcast_in_dim.40), dimensions={1,2} | broadcast | bytes 17408 | tf_op jit(solution)/shard_map/broadcast_in_dim | solution.py:25
  2.9 6.1 %all-to-all-start = ((f32[16,2,128]{2,1,0:T(2,128)}), f32[16,2,128]{2,1,0:T(2,128)S(1)}, u32[]{:S(2)}, u32[]{:S(2)}) async-start(f32[16,2,128]{2,1,0:T(2,128)} %broadcast_in_dim.41), calls=%async_computation | async-start | bytes 32768 | tf_op jit(solution)/shard_map/all_to_all | solution.py:26
  9.1 1.9 %convolution_select_fusion = f32[16,128,128]{2,1,0:T(8,128)S(1)} fusion(pred[128,128]{1,0:T(8,128)(4,1)S(1)} %iota_compare_fusion, f32[16,16]{1,0:T(8,128)S(1)} %copy-done.3, f32[16,16]{1,0:T(8,128)S(1)} %get-tuple-element.7, f32[16,16]{1,0:T(8,128)S(1)} %get-tuple-element.6), kind=kOutput, calls=%fused_computation | convolution fusion | flops 50692096 | bytes 1068032 | tf_op jit(solution)/shard_map/cmi,cmj->cij/dot_general | solution.py:95
  11.1 0.9 %fusion.27 = f32[16,8,128]{2,1,0:T(8,128)S(1)} fusion(bf16[16,8,128]{2,1,0:T(8,128)(2,1)S(1)} %bitcast.30, f32[16,128,128]{2,1,0:T(8,128)S(1)} %convolution_select_fusion), kind=kOutput, calls=%fused_computation.52 | convolution fusion | flops 25165824 | bytes 1146880 | tf_op jit(solution)/shard_map/ckj,cij->cki/dot_general | solution.py:98
  12.0 0.1 mul.199
  12.1 4.6 %all-to-all-done = f32[16,2,128]{2,1,0:T(2,128)S(1)} async-done(((f32[16,2,128]{2,1,0:T(2,128)}), f32[16,2,128]{2,1,0:T(2,128)S(1)}, u32[]{:S(2)}, u32[]{:S(2)}) %all-to-all-start) | async-done | bytes 16416 | tf_op jit(solution)/shard_map/all_to_all | solution.py:26
  16.6 0.1 multiply_reduce_fusion.2
  16.8 0.1 mul.211
  16.8 0.0 copy-start
  16.8 0.0 copy-start.1
  16.8 0.0 copy-start.2
  16.8 0.3 convolution_add_fusion
  17.2 0.0 copy-start.5
  17.2 0.4 copy-done
  17.6 0.0 copy-done.1
  17.6 0.0 copy-done.2
  17.6 0.2 copy-done.5
  17.9 0.1 multiply_reduce_fusion.1
  18.0 30.0 %all_to_all.10 = bf16[32,8,128]{2,1,0:T(8,128)(2,1)S(1)} all-to-all(bf16[32,8,128]{2,1,0:T(8,128)(2,1)S(1)} %broadcast_in_dim.68), channel_id=1, replica_groups=mesh['ctx'=16,'ch'=32] {'ch'}, dimensions={0} | all-to-all | bytes 131072 | tf_op jit(solution)/shard_map/all_to_all | solution.py:26
  48.0 0.0 copy-start.6
  48.0 0.6 %copy-done.6 = f32[16]{0:T(128)S(1)} copy-done((f32[16]{0:T(128)S(1)}, f32[16]{0:T(128)}, u32[]{:S(2)}) %copy-start.6) | copy-done | bytes 88
  48.6 0.7 %multiply_convert_fusion = bf16[16,1024]{1,0:T(8,128)(2,1)} fusion(f32[16]{0:T(128)S(1)} %copy-done.6, f32[1024]{0:T(1024)S(1)} %sqrt_bitcast_fusion, bf16[16,1024]{1,0:T(8,128)(2,1)S(1)} %copy-done, bf16[16,1024]{1,0:T(8,128)(2,1)S(1)} %copy-done.1, f32[16]{0:T(128)S(1)} %copy-done.5, f32[2,8,8,128]{3,2,1,0:T(8,128)S(1)} %bitcast.26, ...), kind=kLoop, calls=%fused_computation.20 | loop fusion | flops 147456 | bytes 200832 | tf_op jit(solution)/shard_map/convert_element_type | solution.py:122
  (14 shorter events, 0.2 us)
Async XLA Ops:
  0.8 0.7 %copy-start.4 = (f32[16,16]{1,0:T(8,128)S(1)}, f32[16,16]{1,0:T(8,128)}, u32[]{:S(2)}) copy-start(f32[16,16]{1,0:T(8,128)} %param.10) | copy-start | bytes 3076
  0.8 0.7 %copy-start.3 = (f32[16,16]{1,0:T(8,128)S(1)}, f32[16,16]{1,0:T(8,128)}, u32[]{:S(2)}) copy-start(f32[16,16]{1,0:T(8,128)} %param.11) | copy-start | bytes 3076
  2.9 13.7 %all-to-all-start = ((f32[16,2,128]{2,1,0:T(2,128)}), f32[16,2,128]{2,1,0:T(2,128)S(1)}, u32[]{:S(2)}, u32[]{:S(2)}) async-start(f32[16,2,128]{2,1,0:T(2,128)} %broadcast_in_dim.41), calls=%async_computation | async-start | bytes 32768 | tf_op jit(solution)/shard_map/all_to_all | solution.py:26
  16.8 0.8 %copy-start = (bf16[16,1024]{1,0:T(8,128)(2,1)S(1)}, bf16[16,1024]{1,0:T(8,128)(2,1)}, u32[]{:S(2)}) copy-start(bf16[16,1024]{1,0:T(8,128)(2,1)} %param.8) | copy-start | bytes 98308
  16.8 0.8 %copy-start.1 = (bf16[16,1024]{1,0:T(8,128)(2,1)S(1)}, bf16[16,1024]{1,0:T(8,128)(2,1)}, u32[]{:S(2)}) copy-start(bf16[16,1024]{1,0:T(8,128)(2,1)} %param.9) | copy-start | bytes 98308
  16.8 0.8 %copy-start.2 = (bf16[16,1024]{1,0:T(8,128)(2,1)S(1)}, bf16[16,1024]{1,0:T(8,128)(2,1)}, u32[]{:S(2)}) copy-start(bf16[16,1024]{1,0:T(8,128)(2,1)} %param.7) | copy-start | bytes 98308
  17.2 0.7 %copy-start.5 = (f32[16]{0:T(128)S(1)}, f32[16]{0:T(128)}, u32[]{:S(2)}) copy-start(f32[16]{0:T(128)} %param.12) | copy-start | bytes 196
  48.0 0.7 %copy-start.6 = (f32[16]{0:T(128)S(1)}, f32[16]{0:T(128)}, u32[]{:S(2)}) copy-start(f32[16]{0:T(128)} %param.13) | copy-start | bytes 196

commit v5 on v4

--- a/solution.py
+++ b/solution.py
@@ -9,6 +9,8 @@
 CH_MODE = "a2a"
 FLAT_STATE = True
 CH_TYPE = jnp.bfloat16
+INNER_FIRST = False
+GAIN_EARLY = True
 
 
 def shifted(block, axis, distance, cyclic=False):
@@ -107,6 +109,8 @@
     local = jnp.einsum("cmkq,cqm->ckm", carry, ends, precision=HI)
     block_state = local[:, chunks, :]
 
+    if INNER_FIRST:
+        block_state, inner = lax.optimization_barrier((block_state, inner))
     before = ctx_state(block_state, rate, float(block_len))
     start = jnp.arange(chunks, dtype=f32)
     entering = jnp.exp(-rate[:, None, :] * (chunk * start)[None, :, None]) * before[:, None, :]
@@ -117,8 +121,13 @@
 
     mixed = query.astype(f32) * (conv + skip[:, None] * sig)
     channel_total = rows * lax.axis_size("ch")
-    square_sum = ch_sum(jnp.sum(mixed * mixed, axis=0))
+    part = jnp.sum(mixed * mixed, axis=0)
+    if GAIN_EARLY:
+        weighted, part = lax.optimization_barrier((mixed * gain[:, None], part))
+    square_sum = ch_sum(part)
     mean_square = square_sum / channel_total
+    if GAIN_EARLY:
+        return (weighted / jnp.sqrt(mean_square + 1e-06)[None, :]).astype(jnp.bfloat16)
     return (mixed / jnp.sqrt(mean_square + 1e-06)[None, :] * gain[:, None]).astype(jnp.bfloat16)
 
 

time: 49.7 us -> 49 us (0.986)
  local copies, waits for them, and re-layouts: 2.82 us -> 2.19 us
    unnamed x15, local copies, waits for them, and re-layouts: 1.93 us -> 1.3 us
where the time goes in v5:
time: 49 us; the launch traced here: 48.7 us
  blocking collectives  30 us (61%)
  starting transfers between devices  6.14 us (13%)
  waiting for transfers between devices  4.56 us (9%)
  matrix products  3.49 us (7%)
  local copies, waits for them, and re-layouts  2.19 us (4%)
  other arithmetic  2.17 us (4%)
    all_to_all x1, blocking collectives, everyone(): return lax.all_to_all(copies, axis, 0, 0, tiled=True)  30 us
    all_to_all x1, starting transfers between devices, everyone(): return lax.all_to_all(copies, axis, 0, 0, tiled=True)  6.14 us
    all_to_all x1, waiting for transfers between devices, everyone(): return lax.all_to_all(copies, axis, 0, 0, tiled=True)  4.56 us
    dot_general x1, matrix products, body(): toeplitz = jnp.einsum('cmi,cmj->cij', fall, rise, precision=HI)  1.93 us
    unnamed x15, local copies, waits for them, and re-layouts  1.3 us
  transfers between devices with their start and end apart: 1, of which 1 were waited for; matrix products, arithmetic and copies ran while one was open for 6% of the time, Pallas kernels for 0%

profile of v5, /device:TPU:2, one launch (start us, length us, event | category | flops | bytes accessed | tf_op | source)
XLA Modules:
  0.0 48.7 jit_solution(10175390444290259055)
XLA Ops:
  0.0 0.8 %multiply_bitcast_fusion = bf16[2,8,8,128]{3,1,2,0:T(8,128)(2,1)S(1)} fusion(bf16[16,1024]{1,0:T(8,128)(2,1)} %param.8, bf16[16,1024]{1,0:T(8,128)(2,1)} %param.9), kind=kLoop, calls=%fused_computation.39 | loop fusion | flops 16384 | bytes 98304
  0.8 0.0 copy-start.4
  0.8 0.0 copy-start.2
  0.8 0.1 convert_multiply_fusion
  0.9 0.6 %copy-done.4 = f32[16,16]{1,0:T(8,128)S(1)} copy-done((f32[16,16]{1,0:T(8,128)S(1)}, f32[16,16]{1,0:T(8,128)}, u32[]{:S(2)}) %copy-start.4) | copy-done | bytes 1048
  1.5 0.0 copy-done.2
  1.5 0.3 convolution_bitcast_fusion
  1.9 0.3 multiply_reduce_fusion
  2.2 0.1 broadcast_in_dim.68
  2.3 0.6 %broadcast_in_dim.69 = f32[16,2,128]{2,1,0:T(2,128)} broadcast(f32[2,128]{1,0:T(2,128)S(1)} %broadcast_in_dim.68), dimensions={1,2} | broadcast | bytes 17408 | tf_op jit(solution)/shard_map/broadcast_in_dim | solution.py:27
  2.9 6.1 %all-to-all-start = ((f32[16,2,128]{2,1,0:T(2,128)}), f32[16,2,128]{2,1,0:T(2,128)S(1)}, u32[]{:S(2)}, u32[]{:S(2)}) async-start(f32[16,2,128]{2,1,0:T(2,128)} %broadcast_in_dim.69), calls=%async_computation | async-start | bytes 32768 | tf_op jit(solution)/shard_map/all_to_all | solution.py:28
  9.1 1.9 %convolution_select_fusion = f32[16,128,128]{2,1,0:T(8,128)S(1)} fusion(pred[128,128]{1,0:T(8,128)(4,1)S(1)} %iota_compare_fusion, f32[16,16]{1,0:T(8,128)S(1)} %copy-done.2, f32[16,16]{1,0:T(8,128)S(1)} %get-tuple-element.13, f32[16,16]{1,0:T(8,128)S(1)} %get-tuple-element.12), kind=kOutput, calls=%fused_computation | convolution fusion | flops 50692096 | bytes 1068032 | tf_op jit(solution)/shard_map/cmi,cmj->cij/dot_general | solution.py:97
  11.1 0.9 %fusion.27 = f32[16,8,128]{2,1,0:T(8,128)S(1)} fusion(bf16[16,8,128]{2,1,0:T(8,128)(2,1)S(1)} %bitcast.28, f32[16,128,128]{2,1,0:T(8,128)S(1)} %convolution_select_fusion), kind=kOutput, calls=%fused_computation.53 | convolution fusion | flops 25165824 | bytes 1146880 | tf_op jit(solution)/shard_map/ckj,cij->cki/dot_general | solution.py:100
  12.0 0.1 mul.199
  12.1 4.6 %all-to-all-done = f32[16,2,128]{2,1,0:T(2,128)S(1)} async-done(((f32[16,2,128]{2,1,0:T(2,128)}), f32[16,2,128]{2,1,0:T(2,128)S(1)}, u32[]{:S(2)}, u32[]{:S(2)}) %all-to-all-start) | async-done | bytes 16416 | tf_op jit(solution)/shard_map/all_to_all | solution.py:28
  16.6 0.1 multiply_reduce_fusion.2
  16.8 0.1 mul.211
  16.8 0.0 copy-start
  16.8 0.0 copy-start.1
  16.8 0.0 copy-start.3
  16.8 0.3 convolution_add_fusion
  17.2 0.0 copy-start.5
  17.2 0.0 copy-start.6
  17.2 0.4 copy-done
  17.6 0.0 copy-done.1
  17.6 0.0 copy-done.3
  17.6 0.2 copy-done.5
  17.9 0.0 copy-done.6
  17.9 0.1 multiply_reduce_fusion.1
  18.0 30.0 %all_to_all.10 = bf16[32,8,128]{2,1,0:T(8,128)(2,1)S(1)} all-to-all(bf16[32,8,128]{2,1,0:T(8,128)(2,1)S(1)} %broadcast_in_dim.71), channel_id=1, replica_groups=mesh['ctx'=16,'ch'=32] {'ch'}, dimensions={0} | all-to-all | bytes 131072 | tf_op jit(solution)/shard_map/all_to_all | solution.py:28
  48.0 0.6 %divide_convert_fusion = bf16[16,1024]{1,0:T(8,128)(2,1)} fusion(f32[16,1024]{1,0:T(8,128)S(1)} %get-tuple-element.7, f32[1024]{0:T(1024)S(1)} %sqrt_bitcast_fusion), kind=kLoop, calls=%fused_computation.20 | loop fusion | flops 32768 | bytes 102400 | tf_op jit(solution)/shard_map/convert_element_type | solution.py:130
  (14 shorter events, 0.2 us)
Async XLA Ops:
  0.8 0.7 %copy-start.4 = (f32[16,16]{1,0:T(8,128)S(1)}, f32[16,16]{1,0:T(8,128)}, u32[]{:S(2)}) copy-start(f32[16,16]{1,0:T(8,128)} %param.10) | copy-start | bytes 3076
  0.8 0.7 %copy-start.2 = (f32[16,16]{1,0:T(8,128)S(1)}, f32[16,16]{1,0:T(8,128)}, u32[]{:S(2)}) copy-start(f32[16,16]{1,0:T(8,128)} %param.11) | copy-start | bytes 3076
  2.9 13.7 %all-to-all-start = ((f32[16,2,128]{2,1,0:T(2,128)}), f32[16,2,128]{2,1,0:T(2,128)S(1)}, u32[]{:S(2)}, u32[]{:S(2)}) async-start(f32[16,2,128]{2,1,0:T(2,128)} %broadcast_in_dim.69), calls=%async_computation | async-start | bytes 32768 | tf_op jit(solution)/shard_map/all_to_all | solution.py:28
  16.8 0.8 %copy-start = (bf16[16,1024]{1,0:T(8,128)(2,1)S(1)}, bf16[16,1024]{1,0:T(8,128)(2,1)}, u32[]{:S(2)}) copy-start(bf16[16,1024]{1,0:T(8,128)(2,1)} %param.8) | copy-start | bytes 98308
  16.8 0.8 %copy-start.1 = (bf16[16,1024]{1,0:T(8,128)(2,1)S(1)}, bf16[16,1024]{1,0:T(8,128)(2,1)}, u32[]{:S(2)}) copy-start(bf16[16,1024]{1,0:T(8,128)(2,1)} %param.9) | copy-start | bytes 98308
  16.8 0.8 %copy-start.3 = (bf16[16,1024]{1,0:T(8,128)(2,1)S(1)}, bf16[16,1024]{1,0:T(8,128)(2,1)}, u32[]{:S(2)}) copy-start(bf16[16,1024]{1,0:T(8,128)(2,1)} %param.7) | copy-start | bytes 98308
  17.2 0.7 %copy-start.5 = (f32[16]{0:T(128)S(1)}, f32[16]{0:T(128)}, u32[]{:S(2)}) copy-start(f32[16]{0:T(128)} %param.12) | copy-start | bytes 196
  17.2 0.7 %copy-start.6 = (f32[16]{0:T(128)S(1)}, f32[16]{0:T(128)}, u32[]{:S(2)}) copy-start(f32[16]{0:T(128)} %param.13) | copy-start | bytes 196

commit v6 on v5

--- a/solution.py
+++ b/solution.py
@@ -10,6 +10,7 @@
 FLAT_STATE = True
 CH_TYPE = jnp.bfloat16
 INNER_FIRST = False
+DIRECT_STATE = "sum"
 GAIN_EARLY = True
 
 
@@ -108,6 +109,13 @@
     carry = jnp.where(earlier < later, carry, 0.0)
     local = jnp.einsum("cmkq,cqm->ckm", carry, ends, precision=HI)
     block_state = local[:, chunks, :]
+    if DIRECT_STATE != "none":
+        spot = jnp.arange(block_len, dtype=f32)
+        decay = jnp.exp(-rate3 * (block_len - 1.0 - spot))
+        if DIRECT_STATE == "sum":
+            block_state = jnp.sum(sig[:, None, :] * decay, axis=2)
+        else:
+            block_state = jnp.einsum("cp,cmp->cm", sig, decay, precision=HI)
 
     if INNER_FIRST:
         block_state, inner = lax.optimization_barrier((block_state, inner))

time: 49 us -> 47.9 us (0.978)
  waiting for transfers between devices: 4.56 us -> 3.79 us
  local copies, waits for them, and re-layouts: 2.19 us -> 1.56 us
    convert_element_type x0 -> x1, other arithmetic: none -> 0.8 us  [body(): sig = signal.astype(f32)]
    unnamed x1 -> x0, other arithmetic: 0.78 us -> none
    all_to_all x1, waiting for transfers between devices: 4.56 us -> 3.79 us  [everyone(): return lax.all_to_all(copies, axis, 0, 0, tiled=True)]
    unnamed x15 -> x11, local copies, waits for them, and re-layouts: 1.3 us -> 0.68 us
  transfers between devices with their start and end apart: 1 -> 1, of which waited for: 1 -> 1; matrix products, arithmetic and copies ran while one was open for 6% -> 8% of each run, Pallas kernels for 0% -> 0%
where the time goes in v6:
time: 47.9 us; the launch traced here: 47.6 us
  blocking collectives  30 us (63%)
  starting transfers between devices  6.14 us (13%)
  waiting for transfers between devices  3.79 us (8%)
  matrix products  3.52 us (7%)
  other arithmetic  2.5 us (5%)
  local copies, waits for them, and re-layouts  1.56 us (3%)
    all_to_all x1, blocking collectives, everyone(): return lax.all_to_all(copies, axis, 0, 0, tiled=True)  30 us
    all_to_all x1, starting transfers between devices, everyone(): return lax.all_to_all(copies, axis, 0, 0, tiled=True)  6.14 us
    all_to_all x1, waiting for transfers between devices, everyone(): return lax.all_to_all(copies, axis, 0, 0, tiled=True)  3.79 us
    dot_general x1, matrix products, body(): toeplitz = jnp.einsum('cmi,cmj->cij', fall, rise, precision=HI)  1.93 us
  transfers between devices with their start and end apart: 1, of which 1 were waited for; matrix products, arithmetic and copies ran while one was open for 8% of the time, Pallas kernels for 0%

profile of v6, /device:TPU:2, one launch (start us, length us, event | category | flops | bytes accessed | tf_op | source)
XLA Modules:
  0.0 47.6 jit_solution(15868226547071010631)
XLA Ops:
  0.0 0.0 copy-start
  0.0 0.0 copy-start.2
  0.0 0.8 %fusion.27 = (f32[16,1024]{1,0:T(8,128)S(1)}, bf16[16,1024]{1,0:T(8,128)(2,1)S(1)}) fusion(bf16[16,1024]{1,0:T(8,128)(2,1)} %param.8, bf16[16,1024]{1,0:T(8,128)(2,1)} %param.9), kind=kLoop, calls=%fused_computation.53 | loop fusion | flops 32768 | bytes 163840 | tf_op jit(solution)/shard_map/convert_element_type | solution.py:88
  0.8 0.0 copy-done
  0.8 0.0 copy-done.2
  0.9 0.3 multiply_reduce_fusion
  1.2 0.1 broadcast_in_dim.40
  1.3 0.6 %broadcast_in_dim.41 = f32[16,2,128]{2,1,0:T(2,128)} broadcast(f32[2,128]{1,0:T(2,128)S(1)} %broadcast_in_dim.40), dimensions={1,2} | broadcast | bytes 17408 | tf_op jit(solution)/shard_map/broadcast_in_dim | solution.py:28
  1.9 6.1 %all-to-all-start = ((f32[16,2,128]{2,1,0:T(2,128)}), f32[16,2,128]{2,1,0:T(2,128)S(1)}, u32[]{:S(2)}, u32[]{:S(2)}) async-start(f32[16,2,128]{2,1,0:T(2,128)} %broadcast_in_dim.41), calls=%async_computation | async-start | bytes 32768 | tf_op jit(solution)/shard_map/all_to_all | solution.py:29
  8.2 1.9 %convolution_select_fusion = f32[16,128,128]{2,1,0:T(8,128)S(1)} fusion(pred[128,128]{1,0:T(8,128)(4,1)S(1)} %iota_compare_fusion, f32[16,16]{1,0:T(8,128)S(1)} %copy-done, f32[16,16]{1,0:T(8,128)S(1)} %get-tuple-element.15, f32[16,16]{1,0:T(8,128)S(1)} %get-tuple-element.14), kind=kOutput, calls=%fused_computation | convolution fusion | flops 50692096 | bytes 1068032 | tf_op jit(solution)/shard_map/cmi,cmj->cij/dot_general | solution.py:98
  10.1 0.9 %fusion.28 = f32[16,8,128]{2,1,0:T(8,128)S(1)} fusion(bf16[16,8,128]{2,1,0:T(8,128)(2,1)S(1)} %bitcast.25, f32[16,128,128]{2,1,0:T(8,128)S(1)} %convolution_select_fusion), kind=kOutput, calls=%fused_computation.54 | convolution fusion | flops 25165824 | bytes 1146880 | tf_op jit(solution)/shard_map/ckj,cij->cki/dot_general | solution.py:101
  11.0 0.3 convolution_bitcast_fusion
  11.3 0.1 convert_multiply_fusion
  11.4 0.3 multiply_reduce_fusion.1
  11.8 0.1 mul.220
  11.8 3.8 %all-to-all-done = f32[16,2,128]{2,1,0:T(2,128)S(1)} async-done(((f32[16,2,128]{2,1,0:T(2,128)}), f32[16,2,128]{2,1,0:T(2,128)S(1)}, u32[]{:S(2)}, u32[]{:S(2)}) %all-to-all-start) | async-done | bytes 16416 | tf_op jit(solution)/shard_map/all_to_all | solution.py:29
  15.6 0.1 multiply_reduce_fusion.3
  15.7 0.1 mul.230
  15.8 0.0 copy-start.1
  15.8 0.4 convolution_add_fusion
  16.2 0.0 copy-start.3
  16.2 0.0 copy-start.4
  16.2 0.4 copy-done.1
  16.6 0.3 copy-done.3
  16.8 0.0 copy-done.4
  16.9 0.1 multiply_reduce_fusion.2
  17.0 30.0 %all_to_all.10 = bf16[32,8,128]{2,1,0:T(8,128)(2,1)S(1)} all-to-all(bf16[32,8,128]{2,1,0:T(8,128)(2,1)S(1)} %broadcast_in_dim.73), channel_id=1, replica_groups=mesh['ctx'=16,'ch'=32] {'ch'}, dimensions={0} | all-to-all | bytes 131072 | tf_op jit(solution)/shard_map/all_to_all | solution.py:29
  47.0 0.6 %divide_convert_fusion = bf16[16,1024]{1,0:T(8,128)(2,1)} fusion(f32[16,1024]{1,0:T(8,128)S(1)} %get-tuple-element.7, f32[1024]{0:T(1024)S(1)} %sqrt_bitcast_fusion), kind=kLoop, calls=%fused_computation.21 | loop fusion | flops 32768 | bytes 102400 | tf_op jit(solution)/shard_map/convert_element_type | solution.py:138
  (14 shorter events, 0.2 us)
Async XLA Ops:
  0.0 0.8 %copy-start = (f32[16,16]{1,0:T(8,128)S(1)}, f32[16,16]{1,0:T(8,128)}, u32[]{:S(2)}) copy-start(f32[16,16]{1,0:T(8,128)} %param.11) | copy-start | bytes 3076
  0.0 0.8 %copy-start.2 = (f32[16,16]{1,0:T(8,128)S(1)}, f32[16,16]{1,0:T(8,128)}, u32[]{:S(2)}) copy-start(f32[16,16]{1,0:T(8,128)} %param.10) | copy-start | bytes 3076
  1.9 13.7 %all-to-all-start = ((f32[16,2,128]{2,1,0:T(2,128)}), f32[16,2,128]{2,1,0:T(2,128)S(1)}, u32[]{:S(2)}, u32[]{:S(2)}) async-start(f32[16,2,128]{2,1,0:T(2,128)} %broadcast_in_dim.41), calls=%async_computation | async-start | bytes 32768 | tf_op jit(solution)/shard_map/all_to_all | solution.py:29
  15.8 0.8 %copy-start.1 = (bf16[16,1024]{1,0:T(8,128)(2,1)S(1)}, bf16[16,1024]{1,0:T(8,128)(2,1)}, u32[]{:S(2)}) copy-start(bf16[16,1024]{1,0:T(8,128)(2,1)} %param.7) | copy-start | bytes 98308
  16.2 0.7 %copy-start.3 = (f32[16]{0:T(128)S(1)}, f32[16]{0:T(128)}, u32[]{:S(2)}) copy-start(f32[16]{0:T(128)} %param.12) | copy-start | bytes 196
  16.2 0.7 %copy-start.4 = (f32[16]{0:T(128)S(1)}, f32[16]{0:T(128)}, u32[]{:S(2)}) copy-start(f32[16]{0:T(128)} %param.13) | copy-start | bytes 196
